TPU v7x, 512 devices: a whole 4x8x8 slice. The times are simulated.
512 devices in a mesh: panel: 64 (over y, z), point: 8 (over x, core).
Axes of the slice: x: 4, y: 8, z: 8, core: 2. Of those that a mesh axis runs over, the one named last changes fastest.
Arguments:
- node_velocity: float32 [2, 1048576], P(None, ('panel', 'point')), may hold values from -1.5 to 1.5
- node_owner: int32 [1048576, 1], P(('panel', 'point')), may hold values from 0 to 63; in each aligned block of 2048 rows (0 to 2047, 2048 to 4095, ...) at most 64 rows name the same one
- node_panel: int32 [1048576], P(('panel', 'point')), may hold values from 0 to 127
- panel_centroid: float32 [3, 8192], P(None, 'panel'), may hold values from -1 to 1
- panel_area: float32 [8192], P('panel'), may hold values from 0.05 to 0.5
- field_points: float32 [3, 65536], P(None, ('panel', 'point')), may hold values from 1.2 to 3
Outputs:
- pressure: float32 [2, 65536], P(None, ('panel', 'point'))
Inputs may be any that keep to these rules, and one draw needn't show every extreme that they name: `node_owner`: among the rows of one device at most 64 name the same owner, a bound that some block reaches.
All inputs are finite; a program needn't handle non-finite values.
Results may differ from a plain program's by a relative error of at most 0.0003.
Values sent between devices are 32-bit elements; how exact they have to be, the bound alone decides.
No kernel may reach another device: no remote copies, remote signals or barrier semaphores. Data moves between devices by JAX's collectives and lax.ppermute only.
A program may use at most 64 MiB of HBM per device.

v0:
```python
import math

import jax
import jax.numpy as jnp
from jax import lax
from jax.experimental import pallas as pl
from jax.experimental.pallas import tpu as pltpu
from jax.sharding import PartitionSpec as P

WAVENUMBER = 40.0
FOUR_PI = 4.0 * math.pi


TWO_OVER_PI = 2.0 / math.pi
HALF_PI_1 = 1.5703125
HALF_PI_2 = 4.837512969970703125e-4
HALF_PI_3 = 7.54978995489188216e-8
GROUP = 16
PARTS_STEP = 8
CONTRACT_STEP = 16


def sine_cosine(angle):
    turns = jnp.floor(angle * TWO_OVER_PI + 0.5)
    rest = ((angle - turns * HALF_PI_1) - turns * HALF_PI_2) - turns * HALF_PI_3
    square = rest * rest
    sine = rest + rest * square * (
        -1.6666654611e-1 + square * (8.3321608736e-3 + square * -1.9515295891e-4)
    )
    cosine = 1.0 - 0.5 * square + square * square * (
        4.166664568298827e-2 + square * (-1.388731625493765e-3 + square * 2.443315711809948e-5)
    )
    quadrant = turns.astype(jnp.int32)
    swap = (quadrant & 1) == 1
    sine_out = jnp.where(swap, cosine, sine)
    cosine_out = jnp.where(swap, sine, cosine)
    sine_out = jnp.where((quadrant & 2) == 2, -sine_out, sine_out)
    cosine_out = jnp.where(((quadrant + 1) & 2) == 2, -cosine_out, cosine_out)
    return sine_out, cosine_out


def green_kernel(panel_ref, point_ref, out_ref, total_ref):
    chunks = panel_ref.shape[0]
    points = point_ref.shape[1]
    for group in range(points // GROUP):
        rows = pl.ds(group * GROUP, GROUP)
        point_x = point_ref[0, rows, :]
        point_y = point_ref[1, rows, :]
        point_z = point_ref[2, rows, :]

        def body(chunk, carry):
            real_sum, imag_sum = carry
            block = panel_ref[chunk]
            shape = (GROUP, block.shape[1])
            strength_re = jnp.broadcast_to(block[0:1], shape)
            strength_im = jnp.broadcast_to(block[1:2], shape)
            delta_x = point_x - jnp.broadcast_to(block[2:3], shape)
            delta_y = point_y - jnp.broadcast_to(block[3:4], shape)
            delta_z = point_z - jnp.broadcast_to(block[4:5], shape)
            distance = jnp.sqrt(delta_x * delta_x + delta_y * delta_y + delta_z * delta_z)
            inverse = 1.0 / (FOUR_PI * distance)
            sine, cosine = sine_cosine(WAVENUMBER * distance)
            cosine_part = cosine * inverse
            sine_part = sine * inverse
            real_sum = real_sum + (strength_re * cosine_part - strength_im * sine_part)
            imag_sum = imag_sum + (strength_re * sine_part + strength_im * cosine_part)
            return real_sum, imag_sum

        zero = jnp.zeros((GROUP, panel_ref.shape[2]), jnp.float32)
        real_sum, imag_sum = lax.fori_loop(0, chunks, body, (zero, zero), unroll=2)
        total_ref[0, rows, :] = real_sum
        total_ref[1, rows, :] = imag_sum
    out_ref[0:1, :] = jnp.sum(total_ref[0].T, axis=0, keepdims=True)
    out_ref[1:2, :] = jnp.sum(total_ref[1].T, axis=0, keepdims=True)


def green(panels, field_points):
    points = field_points.shape[1]
    lanes = panels.shape[2]
    spread = jnp.broadcast_to(field_points[:, :, None], (3, points, lanes))
    pairs = panels.shape[0] * lanes * points
    return pl.pallas_call(
        green_kernel,
        out_shape=jax.ShapeDtypeStruct((2, points), jnp.float32),
        in_specs=[pl.BlockSpec(memory_space=pltpu.VMEM)] * 2,
        out_specs=pl.BlockSpec(memory_space=pltpu.VMEM),
        scratch_shapes=[pltpu.VMEM((2, points, lanes), jnp.float32)],
        cost_estimate=pl.CostEstimate(flops=70 * pairs, transcendentals=2 * pairs, bytes_accessed=4 * (panels.size + spread.size + 2 * points)),
    )(panels, spread)


def parts_kernel(panel_ref, point_ref, cosine_ref, sine_ref):
    points = point_ref.shape[1]

    def body(chunk, carry):
        block = panel_ref[chunk]
        shape = (GROUP, block.shape[1])
        centroid_x = jnp.broadcast_to(block[2:3], shape)
        centroid_y = jnp.broadcast_to(block[3:4], shape)
        centroid_z = jnp.broadcast_to(block[4:5], shape)
        for group in range(points // GROUP):
            rows = pl.ds(group * GROUP, GROUP)
            delta_x = point_ref[0, rows, :] - centroid_x
            delta_y = point_ref[1, rows, :] - centroid_y
            delta_z = point_ref[2, rows, :] - centroid_z
            distance = jnp.sqrt(delta_x * delta_x + delta_y * delta_y + delta_z * delta_z)
            inverse = 1.0 / (FOUR_PI * distance)
            sine, cosine = sine_cosine(WAVENUMBER * distance)
            cosine_ref[chunk, rows, :] = cosine * inverse
            sine_ref[chunk, rows, :] = sine * inverse
        return carry

    lax.fori_loop(0, panel_ref.shape[0], body, 0)


def contract_kernel(strength_ref, cosine_ref, sine_ref, out_ref, real_ref, imag_ref):
    step = pl.program_id(0)

    @pl.when(step == 0)
    def _():
        real_ref[...] = jnp.zeros_like(real_ref)
        imag_ref[...] = jnp.zeros_like(imag_ref)

    def body(chunk, carry):
        block = strength_ref[chunk]
        shape = real_ref.shape
        strength_re = jnp.broadcast_to(block[0:1], shape)
        strength_im = jnp.broadcast_to(block[1:2], shape)
        cosine_part = cosine_ref[chunk]
        sine_part = sine_ref[chunk]
        real_ref[...] += strength_re * cosine_part - strength_im * sine_part
        imag_ref[...] += strength_re * sine_part + strength_im * cosine_part
        return carry

    lax.fori_loop(0, strength_ref.shape[0], body, 0)

    @pl.when(step == pl.num_programs(0) - 1)
    def _():
        out_ref[0:1, :] = jnp.sum(real_ref[...].T, axis=0, keepdims=True)
        out_ref[1:2, :] = jnp.sum(imag_ref[...].T, axis=0, keepdims=True)


def kernel_parts(panels, field_points):
    chunks, rows, lanes = panels.shape
    points = field_points.shape[1]
    spread = jnp.broadcast_to(field_points[:, :, None], (3, points, lanes))
    pairs = chunks * lanes * points
    part = jax.ShapeDtypeStruct((chunks, points, lanes), jnp.float32)
    return pl.pallas_call(
        parts_kernel,
        out_shape=(part, part),
        grid=(chunks // PARTS_STEP,),
        in_specs=[
            pl.BlockSpec((PARTS_STEP, rows, lanes), lambda c: (c, 0, 0)),
            pl.BlockSpec((3, points, lanes), lambda c: (0, 0, 0)),
        ],
        out_specs=[pl.BlockSpec((PARTS_STEP, points, lanes), lambda c: (c, 0, 0))] * 2,
        cost_estimate=pl.CostEstimate(flops=60 * pairs, transcendentals=2 * pairs, bytes_accessed=8 * pairs),
    )(panels, spread)


def contract(strength, cosine_part, sine_part):
    chunks, points, lanes = cosine_part.shape
    return pl.pallas_call(
        contract_kernel,
        out_shape=jax.ShapeDtypeStruct((2, points), jnp.float32),
        grid=(chunks // CONTRACT_STEP,),
        in_specs=[
            pl.BlockSpec((CONTRACT_STEP, 2, lanes), lambda c: (c, 0, 0)),
            pl.BlockSpec((CONTRACT_STEP, points, lanes), lambda c: (c, 0, 0)),
            pl.BlockSpec((CONTRACT_STEP, points, lanes), lambda c: (c, 0, 0)),
        ],
        out_specs=pl.BlockSpec((2, points), lambda c: (0, 0)),
        scratch_shapes=[pltpu.VMEM((points, lanes), jnp.float32)] * 2,
        cost_estimate=pl.CostEstimate(flops=8 * chunks * points * lanes, transcendentals=0, bytes_accessed=8 * chunks * points * lanes),
    )(strength, cosine_part, sine_part)


def shards(node_velocity, node_owner, node_panel, panel_centroid, panel_area, field_points):
    slab_count = lax.axis_size("panel")
    slab_width = panel_area.shape[0]
    destination = node_owner[:, 0]
    owner_hot = (destination[None, :] == jnp.arange(slab_count, dtype=jnp.int32)[:, None]).astype(
        jnp.float32
    )
    weighted = (node_velocity[:, None, :] * owner_hot[None, :, :]).reshape(2 * slab_count, -1)
    panel_hot = (node_panel[:, None] == jnp.arange(slab_width, dtype=jnp.int32)[None, :]).astype(
        jnp.float32
    )
    partial = jnp.dot(
        weighted, panel_hot, precision=lax.Precision.HIGHEST, preferred_element_type=jnp.float32
    )
    partial = partial.reshape(2, slab_count, slab_width).transpose(1, 0, 2)
    centroid_copies = jnp.broadcast_to(panel_centroid[None], (slab_count,) + panel_centroid.shape)
    outgoing = jnp.concatenate([partial, centroid_copies], axis=1)
    got = lax.all_to_all(outgoing, "panel", split_axis=0, concat_axis=0, tiled=True)
    cosine_part, sine_part = kernel_parts(got, field_points)
    column = jnp.sum(got[:, 0:2], axis=0)
    point_count = lax.axis_size("point")
    copies = jnp.broadcast_to(column[None], (point_count,) + column.shape)
    velocity = jnp.sum(lax.all_to_all(copies, "point", split_axis=0, concat_axis=0, tiled=True), axis=0)
    strength = jnp.stack([-panel_area * velocity[1], panel_area * velocity[0]])
    spread = jnp.broadcast_to(strength[None], (slab_count,) + strength.shape)
    gathered = lax.all_to_all(spread, "panel", split_axis=0, concat_axis=0, tiled=True)
    return contract(gathered, cosine_part, sine_part)


def solution(mesh):
    return jax.shard_map(
        shards,
        mesh=mesh,
        in_specs=(
            P(None, ("panel", "point")),
            P(("panel", "point"), None),
            P(("panel", "point")),
            P(None, "panel"),
            P("panel"),
            P(None, ("panel", "point")),
        ),
        out_specs=P(None, ("panel", "point")),
        check_vma=False,
    )
```

profile of v0, /device:TPU:1, one launch (start us, length us, event | category | flops | bytes accessed | tf_op | source)
XLA Modules:
  0.0 69.0 jit_solution(16760049364889973989)
XLA Ops:
  0.0 0.7 %fusion.7 = f32[64,2048]{1,0:T(8,128)S(1)} fusion(s32[2048]{0:T(1024)} %bitcast.20), kind=kLoop, calls=%fused_computation.8 | loop fusion | flops 262144 | bytes 532480 | tf_op jit(solution)/shard_map/convert_element_type | solution.py:183
  0.7 1.6 %fusion = f32[2,64,128]{2,1,0:T(8,128)S(1)} fusion(s32[2048]{0:T(1024)} %param.8, f32[64,2048]{1,0:T(8,128)S(1)} %fusion.7, f32[2,2048]{1,0:T(2,128)} %param.6), kind=kOutput, calls=%fused_computation.1 | convolution fusion | flops 403177472 | bytes 614400 | tf_op jit(solution)/shard_map/dot_general | solution.py:190
  2.3 0.1 copy.15
  2.4 0.7 %broadcast_in_dim.8 = f32[64,3,128]{2,1,0:T(4,128)S(1)} broadcast(f32[3,128]{1,0:T(4,128)} %param.9), dimensions={1,2} | broadcast | bytes 99840 | tf_op jit(solution)/shard_map/broadcast_in_dim | solution.py:194
  3.1 0.1 pad_maximum_fusion
  3.2 29.8 %all_to_all.15.panel_ref = f32[64,5,128]{2,1,0:T(8,128)S(1)} all-to-all(f32[64,5,128]{2,1,0:T(8,128)S(1)} %pad_maximum_fusion), channel_id=1, replica_groups=mesh['panel'=64,'point'=8] {'panel'}, dimensions={0} | all-to-all | bytes 327680 | tf_op jit(solution)/shard_map/all_to_all | solution.py:196
  32.9 0.0 copy-start
  32.9 0.1 slice_reduce_fusion
  33.0 11.8 %all_to_all.16 = f32[8,2,128]{2,1,0:T(2,128)S(1)} all-to-all(f32[8,2,128]{2,1,0:T(2,128)S(1)} %broadcast_in_dim.9), channel_id=1, replica_groups=mesh['panel'=64,'point'=8] {'point'}, dimensions={0} | all-to-all | bytes 16384 | tf_op jit(solution)/shard_map/all_to_all | solution.py:201
  44.8 0.7 fusion.9
  45.4 0.7 broadcast_in_dim.10
  46.1 4.6 %all-to-all-start.2 = ((f32[64,2,128]{2,1,0:T(2,128)}), f32[64,2,128]{2,1,0:T(2,128)S(1)}, u32[]{:S(2)}, u32[]{:S(2)}) async-start(f32[64,2,128]{2,1,0:T(2,128)} %broadcast_in_dim.10), calls=%async_computation.2 | async-start | bytes 131072 | tf_op jit(solution)/shard_map/all_to_all | solution.py:204
  50.7 1.5 %broadcast_in_dim.11.point_ref = f32[3,128,128]{2,1,0:T(8,128)} broadcast(f32[3,128]{1,0:T(4,128)} %param.11), dimensions={0,1} | broadcast | bytes 198144 | tf_op jit(solution)/shard_map/broadcast_in_dim | solution.py:146
  52.2 0.0 copy-done
  52.2 10.9 %shard_map.64 = (f32[64,128,128]{2,1,0:T(8,128)}, f32[64,128,128]{2,1,0:T(8,128)}) custom-call(f32[64,5,128]{2,1,0:T(8,128)} %copy-done, f32[3,128,128]{2,1,0:T(8,128)} %broadcast_in_dim.11.point_ref), custom_call_target="tpu_custom_call" | custom-call | flops 62914560 | bytes 8388608 | tf_op jit(solution)/shard_map/pallas_call | solution.py:149
  63.1 0.0 all-to-all-done.2.strength_ref
  63.1 0.0 copy-start.1
  63.1 0.6 copy-done.1
  63.7 5.3 %shard_map.65 = f32[2,128]{1,0:T(2,128)} custom-call(f32[64,2,128]{2,1,0:T(2,128)} %copy-done.1, f32[64,128,128]{2,1,0:T(8,128)} %get-tuple-element.7.cosine_ref, f32[64,128,128]{2,1,0:T(8,128)} %get-tuple-element.8.sine_ref), custom_call_target="tpu_custom_call" | custom-call | flops 8388608 | bytes 8388608 | tf_op jit(solution)/shard_map/pallas_call | solution.py:164
  (3 shorter events, 0.0 us)
Async XLA Ops:
  32.9 19.3 %copy-start = (f32[64,5,128]{2,1,0:T(8,128)}, f32[64,5,128]{2,1,0:T(8,128)S(1)}, u32[]{:S(2)}) copy-start(f32[64,5,128]{2,1,0:T(8,128)S(1)} %all_to_all.15.panel_ref) | copy-start | bytes 491524
  46.1 17.0 %all-to-all-start.2 = ((f32[64,2,128]{2,1,0:T(2,128)}), f32[64,2,128]{2,1,0:T(2,128)S(1)}, u32[]{:S(2)}, u32[]{:S(2)}) async-start(f32[64,2,128]{2,1,0:T(2,128)} %broadcast_in_dim.10), calls=%async_computation.2 | async-start | bytes 131072 | tf_op jit(solution)/shard_map/all_to_all | solution.py:204
  63.1 0.6 copy-start.1
where the time goes:
time: 69.5 us; the launch traced here: 69 us
  blocking collectives  41.5 us (60%)
  Pallas kernels  16.2 us (23%)
  starting transfers between devices  4.6 us (7%)
  local copies, waits for them, and re-layouts  3.52 us (5%)
  matrix products  1.57 us (2%)
  other arithmetic  1.55 us (2%)
    all_to_all x1, blocking collectives, shards(): lax.all_to_all(outgoing, 'panel', split_axis=0, concat_axis=0, tiled=True)  29.8 us
    all_to_all x1, blocking collectives, shards(): lax.all_to_all(copies, 'point', split_axis=0, concat_axis=0, tiled=True)  11.8 us
    pallas_call x1, Pallas kernels, kernel_parts(): pl.pallas_call(parts_kernel, out_shape=(part, part), grid=(chunks // PART...  10.9 us
    pallas_call x1, Pallas kernels, contract(): pl.pallas_call(contract_kernel, out_shape=jax.ShapeDtypeStruct((2, points...  5.3 us
    all_to_all x1, starting transfers between devices, shards(): lax.all_to_all(spread, 'panel', split_axis=0, concat_axis=0, tiled=True)  4.6 us
    dot_general x1, matrix products, shards(): jnp.dot(weighted, panel_hot, precision=lax.Precision.HIGHEST, preferred_e...  1.57 us
    broadcast_in_dim x1, local copies, waits for them, and re-layouts, kernel_parts(): spread = jnp.broadcast_to(field_points[:, :, None], (3, points, lanes))  1.48 us
  transfers between devices with their start and end apart: 1, of which 0 were waited for; matrix products, arithmetic and copies ran while one was open for 2% of the time, Pallas kernels for 16%

commit v1 on v0

--- a/solution.py
+++ b/solution.py
@@ -17,7 +17,7 @@
 HALF_PI_3 = 7.54978995489188216e-8
 GROUP = 16
 PARTS_STEP = 8
-CONTRACT_STEP = 16
+CONTRACT_GROUPS = 8
 
 
 def sine_cosine(angle):
@@ -113,31 +113,40 @@
     lax.fori_loop(0, panel_ref.shape[0], body, 0)
 
 
-def contract_kernel(strength_ref, cosine_ref, sine_ref, out_ref, real_ref, imag_ref):
-    step = pl.program_id(0)
-
-    @pl.when(step == 0)
-    def _():
-        real_ref[...] = jnp.zeros_like(real_ref)
-        imag_ref[...] = jnp.zeros_like(imag_ref)
+def contract_kernel(strength_ref, cosine_hbm, sine_hbm, out_ref, cosine_buf, sine_buf, real_ref, imag_ref, sems):
+    chunks = cosine_hbm.shape[0]
+    per_group = chunks // CONTRACT_GROUPS
+
+    def copies(group):
+        window = pl.ds(group * per_group, per_group)
+        return (
+            pltpu.make_async_copy(cosine_hbm.at[window], cosine_buf.at[window], sems.at[0, group]),
+            pltpu.make_async_copy(sine_hbm.at[window], sine_buf.at[window], sems.at[1, group]),
+        )
+
+    for group in range(CONTRACT_GROUPS):
+        for copy in copies(group):
+            copy.start()
+    real_ref[...] = jnp.zeros_like(real_ref)
+    imag_ref[...] = jnp.zeros_like(imag_ref)
 
     def body(chunk, carry):
         block = strength_ref[chunk]
         shape = real_ref.shape
         strength_re = jnp.broadcast_to(block[0:1], shape)
         strength_im = jnp.broadcast_to(block[1:2], shape)
-        cosine_part = cosine_ref[chunk]
-        sine_part = sine_ref[chunk]
+        cosine_part = cosine_buf[chunk]
+        sine_part = sine_buf[chunk]
         real_ref[...] += strength_re * cosine_part - strength_im * sine_part
         imag_ref[...] += strength_re * sine_part + strength_im * cosine_part
         return carry
 
-    lax.fori_loop(0, strength_ref.shape[0], body, 0)
-
-    @pl.when(step == pl.num_programs(0) - 1)
-    def _():
-        out_ref[0:1, :] = jnp.sum(real_ref[...].T, axis=0, keepdims=True)
-        out_ref[1:2, :] = jnp.sum(imag_ref[...].T, axis=0, keepdims=True)
+    for group in range(CONTRACT_GROUPS):
+        for copy in copies(group):
+            copy.wait()
+        lax.fori_loop(group * per_group, (group + 1) * per_group, body, 0)
+    out_ref[0:1, :] = jnp.sum(real_ref[...].T, axis=0, keepdims=True)
+    out_ref[1:2, :] = jnp.sum(imag_ref[...].T, axis=0, keepdims=True)
 
 
 def kernel_parts(panels, field_points):
@@ -164,14 +173,15 @@
     return pl.pallas_call(
         contract_kernel,
         out_shape=jax.ShapeDtypeStruct((2, points), jnp.float32),
-        grid=(chunks // CONTRACT_STEP,),
         in_specs=[
-            pl.BlockSpec((CONTRACT_STEP, 2, lanes), lambda c: (c, 0, 0)),
-            pl.BlockSpec((CONTRACT_STEP, points, lanes), lambda c: (c, 0, 0)),
-            pl.BlockSpec((CONTRACT_STEP, points, lanes), lambda c: (c, 0, 0)),
+            pl.BlockSpec(memory_space=pltpu.VMEM),
+            pl.BlockSpec(memory_space=pl.ANY),
+            pl.BlockSpec(memory_space=pl.ANY),
         ],
-        out_specs=pl.BlockSpec((2, points), lambda c: (0, 0)),
-        scratch_shapes=[pltpu.VMEM((points, lanes), jnp.float32)] * 2,
+        out_specs=pl.BlockSpec(memory_space=pltpu.VMEM),
+        scratch_shapes=[pltpu.VMEM((chunks, points, lanes), jnp.float32)] * 2
+        + [pltpu.VMEM((points, lanes), jnp.float32)] * 2
+        + [pltpu.SemaphoreType.DMA((2, CONTRACT_GROUPS))],
         cost_estimate=pl.CostEstimate(flops=8 * chunks * points * lanes, transcendentals=0, bytes_accessed=8 * chunks * points * lanes),
     )(strength, cosine_part, sine_part)
 

time: 69.5 us -> 69.4 us (level)
  no operation moved by 1% of the time
where the time goes in v1:
time: 69.4 us; the launch traced here: 68.9 us
  blocking collectives  41.5 us (60%)
  Pallas kernels  16.1 us (23%)
  starting transfers between devices  4.6 us (7%)
  local copies, waits for them, and re-layouts  3.52 us (5%)
  matrix products  1.57 us (2%)
  other arithmetic  1.55 us (2%)
    all_to_all x1, blocking collectives, shards(): lax.all_to_all(outgoing, 'panel', split_axis=0, concat_axis=0, tiled=True)  29.8 us
    all_to_all x1, blocking collectives, shards(): lax.all_to_all(copies, 'point', split_axis=0, concat_axis=0, tiled=True)  11.8 us
    pallas_call x1, Pallas kernels, kernel_parts(): pl.pallas_call(parts_kernel, out_shape=(part, part), grid=(chunks // PART...  10.9 us
    pallas_call x1, Pallas kernels, contract(): pl.pallas_call(contract_kernel, out_shape=jax.ShapeDtypeStruct((2, points...  5.2 us
    all_to_all x1, starting transfers between devices, shards(): lax.all_to_all(spread, 'panel', split_axis=0, concat_axis=0, tiled=True)  4.6 us
    dot_general x1, matrix products, shards(): jnp.dot(weighted, panel_hot, precision=lax.Precision.HIGHEST, preferred_e...  1.57 us
    broadcast_in_dim x1, local copies, waits for them, and re-layouts, kernel_parts(): spread = jnp.broadcast_to(field_points[:, :, None], (3, points, lanes))  1.48 us
  transfers between devices with their start and end apart: 1, of which 0 were waited for; matrix products, arithmetic and copies ran while one was open for 2% of the time, Pallas kernels for 16%

profile of v1, /device:TPU:1, one launch (start us, length us, event | category | flops | bytes accessed | tf_op | source)
XLA Modules:
  0.0 68.9 jit_solution(7869883422033696180)
XLA Ops:
  0.0 0.7 %fusion.7 = f32[64,2048]{1,0:T(8,128)S(1)} fusion(s32[2048]{0:T(1024)} %bitcast.20), kind=kLoop, calls=%fused_computation.8 | loop fusion | flops 262144 | bytes 532480 | tf_op jit(solution)/shard_map/convert_element_type | solution.py:193
  0.7 1.6 %fusion = f32[2,64,128]{2,1,0:T(8,128)S(1)} fusion(s32[2048]{0:T(1024)} %param.8, f32[64,2048]{1,0:T(8,128)S(1)} %fusion.7, f32[2,2048]{1,0:T(2,128)} %param.6), kind=kOutput, calls=%fused_computation.1 | convolution fusion | flops 403177472 | bytes 614400 | tf_op jit(solution)/shard_map/dot_general | solution.py:200
  2.3 0.1 copy.15
  2.4 0.7 %broadcast_in_dim.8 = f32[64,3,128]{2,1,0:T(4,128)S(1)} broadcast(f32[3,128]{1,0:T(4,128)} %param.9), dimensions={1,2} | broadcast | bytes 99840 | tf_op jit(solution)/shard_map/broadcast_in_dim | solution.py:204
  3.1 0.1 pad_maximum_fusion
  3.2 29.8 %all_to_all.15.panel_ref = f32[64,5,128]{2,1,0:T(8,128)S(1)} all-to-all(f32[64,5,128]{2,1,0:T(8,128)S(1)} %pad_maximum_fusion), channel_id=1, replica_groups=mesh['panel'=64,'point'=8] {'panel'}, dimensions={0} | all-to-all | bytes 327680 | tf_op jit(solution)/shard_map/all_to_all | solution.py:206
  32.9 0.0 copy-start
  32.9 0.1 slice_reduce_fusion
  33.0 11.8 %all_to_all.16 = f32[8,2,128]{2,1,0:T(2,128)S(1)} all-to-all(f32[8,2,128]{2,1,0:T(2,128)S(1)} %broadcast_in_dim.9), channel_id=1, replica_groups=mesh['panel'=64,'point'=8] {'point'}, dimensions={0} | all-to-all | bytes 16384 | tf_op jit(solution)/shard_map/all_to_all | solution.py:211
  44.8 0.7 fusion.9
  45.4 0.7 broadcast_in_dim.10
  46.1 4.6 %all-to-all-start.2 = ((f32[64,2,128]{2,1,0:T(2,128)}), f32[64,2,128]{2,1,0:T(2,128)S(1)}, u32[]{:S(2)}, u32[]{:S(2)}) async-start(f32[64,2,128]{2,1,0:T(2,128)} %broadcast_in_dim.10), calls=%async_computation.2 | async-start | bytes 131072 | tf_op jit(solution)/shard_map/all_to_all | solution.py:214
  50.7 1.5 %broadcast_in_dim.11.point_ref = f32[3,128,128]{2,1,0:T(8,128)} broadcast(f32[3,128]{1,0:T(4,128)} %param.11), dimensions={0,1} | broadcast | bytes 198144 | tf_op jit(solution)/shard_map/broadcast_in_dim | solution.py:155
  52.2 0.0 copy-done
  52.2 10.9 %shard_map.64 = (f32[64,128,128]{2,1,0:T(8,128)}, f32[64,128,128]{2,1,0:T(8,128)}) custom-call(f32[64,5,128]{2,1,0:T(8,128)} %copy-done, f32[3,128,128]{2,1,0:T(8,128)} %broadcast_in_dim.11.point_ref), custom_call_target="tpu_custom_call" | custom-call | flops 62914560 | bytes 8388608 | tf_op jit(solution)/shard_map/pallas_call | solution.py:158
  63.1 0.0 all-to-all-done.2.strength_ref
  63.1 0.0 copy-start.1
  63.1 0.6 copy-done.1
  63.7 5.2 %shard_map.65 = f32[2,128]{1,0:T(2,128)} custom-call(f32[64,2,128]{2,1,0:T(2,128)} %copy-done.1, f32[64,128,128]{2,1,0:T(8,128)} %get-tuple-element.7.cosine_hbm, f32[64,128,128]{2,1,0:T(8,128)} %get-tuple-element.8.sine_hbm), custom_call_target="tpu_custom_call" | custom-call | flops 8388608 | bytes 8388608 | tf_op jit(solution)/shard_map/pallas_call | solution.py:173
  (3 shorter events, 0.0 us)
Async XLA Ops:
  32.9 19.3 %copy-start = (f32[64,5,128]{2,1,0:T(8,128)}, f32[64,5,128]{2,1,0:T(8,128)S(1)}, u32[]{:S(2)}) copy-start(f32[64,5,128]{2,1,0:T(8,128)S(1)} %all_to_all.15.panel_ref) | copy-start | bytes 491524
  46.1 17.0 %all-to-all-start.2 = ((f32[64,2,128]{2,1,0:T(2,128)}), f32[64,2,128]{2,1,0:T(2,128)S(1)}, u32[]{:S(2)}, u32[]{:S(2)}) async-start(f32[64,2,128]{2,1,0:T(2,128)} %broadcast_in_dim.10), calls=%async_computation.2 | async-start | bytes 131072 | tf_op jit(solution)/shard_map/all_to_all | solution.py:214
  63.1 0.6 copy-start.1

commit v2 on v0

--- a/solution.py
+++ b/solution.py
@@ -197,8 +197,12 @@
     cosine_part, sine_part = kernel_parts(got, field_points)
     column = jnp.sum(got[:, 0:2], axis=0)
     point_count = lax.axis_size("point")
-    copies = jnp.broadcast_to(column[None], (point_count,) + column.shape)
-    velocity = jnp.sum(lax.all_to_all(copies, "point", split_axis=0, concat_axis=0, tiled=True), axis=0)
+    velocity = column
+    distance = 1
+    while distance < point_count:
+        pairs = [(source, source ^ distance) for source in range(point_count)]
+        velocity = velocity + lax.ppermute(velocity, "point", pairs)
+        distance *= 2
     strength = jnp.stack([-panel_area * velocity[1], panel_area * velocity[0]])
     spread = jnp.broadcast_to(strength[None], (slab_count,) + strength.shape)
     gathered = lax.all_to_all(spread, "panel", split_axis=0, concat_axis=0, tiled=True)

time: 69.5 us -> 74.8 us (1.076)
  the two profiles are of different devices: /device:TPU:1 before, /device:TPU:2 now
where the time goes in v2:
time: 74.8 us; the launch traced here: 74.3 us
  blocking collectives  31.3 us (42%)
  Pallas kernels  16.2 us (22%)
  starting transfers between devices  12.9 us (17%)
  waiting for transfers between devices  7.09 us (9%)
  local copies, waits for them, and re-layouts  3.52 us (5%)
  matrix products  1.57 us (2%)
  other arithmetic  1.54 us (2%)
    all_to_all x1, blocking collectives, shards(): lax.all_to_all(outgoing, 'panel', split_axis=0, concat_axis=0, tiled=True)  31.3 us
    pallas_call x1, Pallas kernels, kernel_parts(): pl.pallas_call(parts_kernel, out_shape=(part, part), grid=(chunks // PART...  11 us
    ppermute x3, starting transfers between devices, shards(): velocity = velocity + lax.ppermute(velocity, 'point', pairs)  8.35 us
    ppermute x3, waiting for transfers between devices, shards(): velocity = velocity + lax.ppermute(velocity, 'point', pairs)  7.09 us
    pallas_call x1, Pallas kernels, contract(): pl.pallas_call(contract_kernel, out_shape=jax.ShapeDtypeStruct((2, points...  5.3 us
    all_to_all x1, starting transfers between devices, shards(): lax.all_to_all(spread, 'panel', split_axis=0, concat_axis=0, tiled=True)  4.6 us
    dot_general x1, matrix products, shards(): jnp.dot(weighted, panel_hot, precision=lax.Precision.HIGHEST, preferred_e...  1.57 us
  transfers between devices with their start and end apart: 4, of which 3 were waited for; matrix products, arithmetic and copies ran while one was open for 2% of the time, Pallas kernels for 15%

profile of v2, /device:TPU:2, one launch (start us, length us, event | category | flops | bytes accessed | tf_op | source)
XLA Modules:
  0.0 74.3 jit_solution(680775720123904044)
XLA Ops:
  0.0 0.7 fusion.7
  0.7 1.6 %fusion = f32[2,64,128]{2,1,0:T(8,128)S(1)} fusion(s32[2048]{0:T(1024)} %param.8, f32[64,2048]{1,0:T(8,128)S(1)} %fusion.7, f32[2,2048]{1,0:T(2,128)} %param.6), kind=kOutput, calls=%fused_computation.1 | convolution fusion | flops 403177472 | bytes 614400 | tf_op jit(solution)/shard_map/dot_general | solution.py:190
  2.3 0.1 copy.9
  2.4 0.7 broadcast_in_dim.6
  3.1 0.1 pad_maximum_fusion
  3.2 31.3 %all_to_all.10.panel_ref = f32[64,5,128]{2,1,0:T(8,128)S(1)} all-to-all(f32[64,5,128]{2,1,0:T(8,128)S(1)} %pad_maximum_fusion), channel_id=1, replica_groups=mesh['panel'=64,'point'=8] {'panel'}, dimensions={0} | all-to-all | bytes 327680 | tf_op jit(solution)/shard_map/all_to_all | solution.py:196
  34.5 0.0 copy-start
  34.5 0.1 slice_reduce_fusion
  34.5 1.9 %collective-permute-start = (f32[2,128]{1,0:T(2,128)S(1)}, f32[2,128]{1,0:T(2,128)S(1)}, u32[]{:S(2)}, u32[]{:S(2)}) collective-permute-start(f32[2,128]{1,0:T(2,128)S(1)} %slice_reduce_fusion), channel_id=1, source_target_pairs={{0,1},{1,0},{2,3},{3,2},{4,5},{5,4},{6,7},{7,6},{8,9},{9,8},{10,11... | collective-permute-start | bytes 3080 | tf_op jit(solution)/shard_map/ppermute | solution.py:204
  36.5 1.1 %collective-permute-done = f32[2,128]{1,0:T(2,128)S(1)} collective-permute-done((f32[2,128]{1,0:T(2,128)S(1)}, f32[2,128]{1,0:T(2,128)S(1)}, u32[]{:S(2)}, u32[]{:S(2)}) %collective-permute-start) | collective-permute-done | bytes 1056 | tf_op jit(solution)/shard_map/ppermute | solution.py:204
  37.6 2.4 %collective-permute-start.1 = (f32[2,128]{1,0:T(2,128)S(1)}, f32[2,128]{1,0:T(2,128)S(1)}, u32[]{:S(2)}, u32[]{:S(2)}) collective-permute-start(f32[2,128]{1,0:T(2,128)S(1)} %add.9), channel_id=1, source_target_pairs={{0,2},{1,3},{2,0},{3,1},{4,6},{5,7},{6,4},{7,5},{8,10},{9,11},{10,... | collective-permute-start | bytes 3080 | tf_op jit(solution)/shard_map/ppermute | solution.py:204
  40.0 3.0 %collective-permute-done.1 = f32[2,128]{1,0:T(2,128)S(1)} collective-permute-done((f32[2,128]{1,0:T(2,128)S(1)}, f32[2,128]{1,0:T(2,128)S(1)}, u32[]{:S(2)}, u32[]{:S(2)}) %collective-permute-start.1) | collective-permute-done | bytes 1056 | tf_op jit(solution)/shard_map/ppermute | solution.py:204
  43.1 4.0 %collective-permute-start.2 = (f32[2,128]{1,0:T(2,128)S(1)}, f32[2,128]{1,0:T(2,128)S(1)}, u32[]{:S(2)}, u32[]{:S(2)}) collective-permute-start(f32[2,128]{1,0:T(2,128)S(1)} %add.10), channel_id=1, source_target_pairs={{0,4},{1,5},{2,6},{3,7},{4,0},{5,1},{6,2},{7,3},{8,12},{9,13},{10,... | collective-permute-start | bytes 3080 | tf_op jit(solution)/shard_map/ppermute | solution.py:204
  47.1 2.9 %collective-permute-done.2 = f32[2,128]{1,0:T(2,128)S(1)} collective-permute-done((f32[2,128]{1,0:T(2,128)S(1)}, f32[2,128]{1,0:T(2,128)S(1)}, u32[]{:S(2)}, u32[]{:S(2)}) %collective-permute-start.2) | collective-permute-done | bytes 1056 | tf_op jit(solution)/shard_map/ppermute | solution.py:204
  50.0 0.7 fusion.9
  50.7 0.7 broadcast_in_dim.7
  51.3 4.6 %all-to-all-start.1 = ((f32[64,2,128]{2,1,0:T(2,128)}), f32[64,2,128]{2,1,0:T(2,128)S(1)}, u32[]{:S(2)}, u32[]{:S(2)}) async-start(f32[64,2,128]{2,1,0:T(2,128)} %broadcast_in_dim.7), calls=%async_computation.1 | async-start | bytes 131072 | tf_op jit(solution)/shard_map/all_to_all | solution.py:208
  56.0 1.5 %broadcast_in_dim.8.point_ref = f32[3,128,128]{2,1,0:T(8,128)} broadcast(f32[3,128]{1,0:T(4,128)} %param.11), dimensions={0,1} | broadcast | bytes 198144 | tf_op jit(solution)/shard_map/broadcast_in_dim | solution.py:146
  57.4 0.0 copy-done
  57.4 11.0 %shard_map.64 = (f32[64,128,128]{2,1,0:T(8,128)}, f32[64,128,128]{2,1,0:T(8,128)}) custom-call(f32[64,5,128]{2,1,0:T(8,128)} %copy-done, f32[3,128,128]{2,1,0:T(8,128)} %broadcast_in_dim.8.point_ref), custom_call_target="tpu_custom_call" | custom-call | flops 62914560 | bytes 8388608 | tf_op jit(solution)/shard_map/pallas_call | solution.py:149
  68.4 0.0 all-to-all-done.1.strength_ref
  68.4 0.0 copy-start.1
  68.4 0.6 copy-done.1
  69.0 5.3 %shard_map.65 = f32[2,128]{1,0:T(2,128)} custom-call(f32[64,2,128]{2,1,0:T(2,128)} %copy-done.1, f32[64,128,128]{2,1,0:T(8,128)} %get-tuple-element.7.cosine_ref, f32[64,128,128]{2,1,0:T(8,128)} %get-tuple-element.8.sine_ref), custom_call_target="tpu_custom_call" | custom-call | flops 8388608 | bytes 8388608 | tf_op jit(solution)/shard_map/pallas_call | solution.py:164
  (4 shorter events, 0.0 us)
Async XLA Ops:
  34.5 23.0 %copy-start = (f32[64,5,128]{2,1,0:T(8,128)}, f32[64,5,128]{2,1,0:T(8,128)S(1)}, u32[]{:S(2)}) copy-start(f32[64,5,128]{2,1,0:T(8,128)S(1)} %all_to_all.10.panel_ref) | copy-start | bytes 491524
  34.5 3.0 %collective-permute-start = (f32[2,128]{1,0:T(2,128)S(1)}, f32[2,128]{1,0:T(2,128)S(1)}, u32[]{:S(2)}, u32[]{:S(2)}) collective-permute-start(f32[2,128]{1,0:T(2,128)S(1)} %slice_reduce_fusion), channel_id=1, source_target_pairs={{0,1},{1,0},{2,3},{3,2},{4,5},{5,4},{6,7},{7,6},{8,9},{9,8},{10,11... | collective-permute-start | bytes 3080 | tf_op jit(solution)/shard_map/ppermute | solution.py:204
  37.6 5.5 %collective-permute-start.1 = (f32[2,128]{1,0:T(2,128)S(1)}, f32[2,128]{1,0:T(2,128)S(1)}, u32[]{:S(2)}, u32[]{:S(2)}) collective-permute-start(f32[2,128]{1,0:T(2,128)S(1)} %add.9), channel_id=1, source_target_pairs={{0,2},{1,3},{2,0},{3,1},{4,6},{5,7},{6,4},{7,5},{8,10},{9,11},{10,... | collective-permute-start | bytes 3080 | tf_op jit(solution)/shard_map/ppermute | solution.py:204
  43.1 7.0 %collective-permute-start.2 = (f32[2,128]{1,0:T(2,128)S(1)}, f32[2,128]{1,0:T(2,128)S(1)}, u32[]{:S(2)}, u32[]{:S(2)}) collective-permute-start(f32[2,128]{1,0:T(2,128)S(1)} %add.10), channel_id=1, source_target_pairs={{0,4},{1,5},{2,6},{3,7},{4,0},{5,1},{6,2},{7,3},{8,12},{9,13},{10,... | collective-permute-start | bytes 3080 | tf_op jit(solution)/shard_map/ppermute | solution.py:204
  51.3 17.0 %all-to-all-start.1 = ((f32[64,2,128]{2,1,0:T(2,128)}), f32[64,2,128]{2,1,0:T(2,128)S(1)}, u32[]{:S(2)}, u32[]{:S(2)}) async-start(f32[64,2,128]{2,1,0:T(2,128)} %broadcast_in_dim.7), calls=%async_computation.1 | async-start | bytes 131072 | tf_op jit(solution)/shard_map/all_to_all | solution.py:208
  68.4 0.6 copy-start.1

commit v3 on v0

--- a/solution.py
+++ b/solution.py
@@ -113,8 +113,9 @@
     lax.fori_loop(0, panel_ref.shape[0], body, 0)
 
 
-def contract_kernel(strength_ref, cosine_ref, sine_ref, out_ref, real_ref, imag_ref):
+def contract_kernel(velocity_ref, area_ref, cosine_ref, sine_ref, out_ref, real_ref, imag_ref):
     step = pl.program_id(0)
+    per_step = cosine_ref.shape[0]
 
     @pl.when(step == 0)
     def _():
@@ -122,17 +123,19 @@
         imag_ref[...] = jnp.zeros_like(imag_ref)
 
     def body(chunk, carry):
-        block = strength_ref[chunk]
+        panel_chunk = step * per_step + chunk
+        velocity = velocity_ref[panel_chunk]
+        area = area_ref[panel_chunk]
         shape = real_ref.shape
-        strength_re = jnp.broadcast_to(block[0:1], shape)
-        strength_im = jnp.broadcast_to(block[1:2], shape)
+        strength_re = jnp.broadcast_to(-area[0:1] * velocity[1:2], shape)
+        strength_im = jnp.broadcast_to(area[0:1] * velocity[0:1], shape)
         cosine_part = cosine_ref[chunk]
         sine_part = sine_ref[chunk]
         real_ref[...] += strength_re * cosine_part - strength_im * sine_part
         imag_ref[...] += strength_re * sine_part + strength_im * cosine_part
         return carry
 
-    lax.fori_loop(0, strength_ref.shape[0], body, 0)
+    lax.fori_loop(0, per_step, body, 0)
 
     @pl.when(step == pl.num_programs(0) - 1)
     def _():
@@ -159,21 +162,27 @@
     )(panels, spread)
 
 
-def contract(strength, cosine_part, sine_part):
+def contract(velocity, area, cosine_part, sine_part):
     chunks, points, lanes = cosine_part.shape
     return pl.pallas_call(
         contract_kernel,
         out_shape=jax.ShapeDtypeStruct((2, points), jnp.float32),
         grid=(chunks // CONTRACT_STEP,),
         in_specs=[
-            pl.BlockSpec((CONTRACT_STEP, 2, lanes), lambda c: (c, 0, 0)),
+            pl.BlockSpec(memory_space=pltpu.VMEM),
+            pl.BlockSpec(memory_space=pltpu.VMEM),
             pl.BlockSpec((CONTRACT_STEP, points, lanes), lambda c: (c, 0, 0)),
             pl.BlockSpec((CONTRACT_STEP, points, lanes), lambda c: (c, 0, 0)),
         ],
         out_specs=pl.BlockSpec((2, points), lambda c: (0, 0)),
         scratch_shapes=[pltpu.VMEM((points, lanes), jnp.float32)] * 2,
         cost_estimate=pl.CostEstimate(flops=8 * chunks * points * lanes, transcendentals=0, bytes_accessed=8 * chunks * points * lanes),
-    )(strength, cosine_part, sine_part)
+    )(
+        pltpu.with_memory_space_constraint(velocity, pltpu.VMEM),
+        pltpu.with_memory_space_constraint(area, pltpu.VMEM),
+        cosine_part,
+        sine_part,
+    )
 
 
 def shards(node_velocity, node_owner, node_panel, panel_centroid, panel_area, field_points):
@@ -191,18 +200,18 @@
         weighted, panel_hot, precision=lax.Precision.HIGHEST, preferred_element_type=jnp.float32
     )
     partial = partial.reshape(2, slab_count, slab_width).transpose(1, 0, 2)
-    centroid_copies = jnp.broadcast_to(panel_centroid[None], (slab_count,) + panel_centroid.shape)
-    outgoing = jnp.concatenate([partial, centroid_copies], axis=1)
+    extra = jnp.concatenate([panel_centroid, panel_area[None]], axis=0)
+    extra_copies = jnp.broadcast_to(extra[None], (slab_count,) + extra.shape)
+    outgoing = jnp.concatenate([partial, extra_copies], axis=1)
     got = lax.all_to_all(outgoing, "panel", split_axis=0, concat_axis=0, tiled=True)
     cosine_part, sine_part = kernel_parts(got, field_points)
     column = jnp.sum(got[:, 0:2], axis=0)
     point_count = lax.axis_size("point")
     copies = jnp.broadcast_to(column[None], (point_count,) + column.shape)
     velocity = jnp.sum(lax.all_to_all(copies, "point", split_axis=0, concat_axis=0, tiled=True), axis=0)
-    strength = jnp.stack([-panel_area * velocity[1], panel_area * velocity[0]])
-    spread = jnp.broadcast_to(strength[None], (slab_count,) + strength.shape)
+    spread = jnp.broadcast_to(velocity[None], (slab_count,) + velocity.shape)
     gathered = lax.all_to_all(spread, "panel", split_axis=0, concat_axis=0, tiled=True)
-    return contract(gathered, cosine_part, sine_part)
+    return contract(gathered, got[:, 5:6], cosine_part, sine_part)
 
 
 def solution(mesh):

time: 69.5 us -> 68.4 us (0.984)
  local copies, waits for them, and re-layouts: 3.52 us -> 2.24 us
    concatenate x1 -> x2, other arithmetic: 0.06 us -> 0.76 us  [the longest x1 0.71 us: shards(): extra = jnp.concatenate([panel_centroid, panel_area[None]], axis=0)]
    broadcast_in_dim x2, local copies, waits for them, and re-layouts: 1.35 us -> 0.66 us  [the longest x1 0.64 us: shards(): spread = jnp.broadcast_to(velocity[None], (slab_count,) + velocity.shape)]
where the time goes in v3:
time: 68.4 us; the launch traced here: 67.9 us
  blocking collectives  41.5 us (61%)
  Pallas kernels  16.3 us (24%)
  starting transfers between devices  4.6 us (7%)
  local copies, waits for them, and re-layouts  2.24 us (3%)
  other arithmetic  1.59 us (2%)
  matrix products  1.57 us (2%)
    all_to_all x1, blocking collectives, shards(): lax.all_to_all(outgoing, 'panel', split_axis=0, concat_axis=0, tiled=True)  29.8 us
    all_to_all x1, blocking collectives, shards(): lax.all_to_all(copies, 'point', split_axis=0, concat_axis=0, tiled=True)  11.8 us
    pallas_call x1, Pallas kernels, kernel_parts(): pl.pallas_call(parts_kernel, out_shape=(part, part), grid=(chunks // PART...  10.9 us
    pallas_call x1, Pallas kernels, contract(): pl.pallas_call(contract_kernel, out_shape=jax.ShapeDtypeStruct((2, points...  5.43 us
    all_to_all x1, starting transfers between devices, shards(): lax.all_to_all(spread, 'panel', split_axis=0, concat_axis=0, tiled=True)  4.6 us
    dot_general x1, matrix products, shards(): jnp.dot(weighted, panel_hot, precision=lax.Precision.HIGHEST, preferred_e...  1.57 us
    broadcast_in_dim x1, local copies, waits for them, and re-layouts, kernel_parts(): spread = jnp.broadcast_to(field_points[:, :, None], (3, points, lanes))  1.48 us
  transfers between devices with their start and end apart: 1, of which 0 were waited for; matrix products, arithmetic and copies ran while one was open for 2% of the time, Pallas kernels for 16%

profile of v3, /device:TPU:1, one launch (start us, length us, event | category | flops | bytes accessed | tf_op | source)
XLA Modules:
  0.0 67.9 jit_solution(7802701021198971162)
XLA Ops:
  0.0 0.7 %fusion.7 = f32[64,2048]{1,0:T(8,128)S(1)} fusion(s32[2048]{0:T(1024)} %bitcast.9), kind=kLoop, calls=%fused_computation.8 | loop fusion | flops 262144 | bytes 532480 | tf_op jit(solution)/shard_map/convert_element_type | solution.py:192
  0.7 1.6 %fusion = f32[2,64,128]{2,1,0:T(8,128)S(1)} fusion(s32[2048]{0:T(1024)} %param.8, f32[64,2048]{1,0:T(8,128)S(1)} %fusion.7, f32[2,2048]{1,0:T(2,128)} %param.6), kind=kOutput, calls=%fused_computation.1 | convolution fusion | flops 403177472 | bytes 614400 | tf_op jit(solution)/shard_map/dot_general | solution.py:199
  2.3 0.1 copy.13
  2.4 0.7 %pad_maximum_fusion.1 = f32[4,128]{1,0:T(4,128)S(1)} fusion(f32[1,128]{1,0:T(1,128)} %bitcast.10, f32[3,128]{1,0:T(4,128)} %param.9), kind=kLoop, calls=%fused_computation.12 | loop fusion | flops 512 | bytes 4096 | tf_op jit(solution)/shard_map/concatenate | solution.py:203
  3.1 0.1 pad_maximum_fusion
  3.2 29.8 %all_to_all.15.panel_ref = f32[64,6,128]{2,1,0:T(8,128)S(1)} all-to-all(f32[64,6,128]{2,1,0:T(8,128)S(1)} %pad_maximum_fusion), channel_id=1, replica_groups=mesh['panel'=64,'point'=8] {'panel'}, dimensions={0} | all-to-all | bytes 393216 | tf_op jit(solution)/shard_map/all_to_all | solution.py:206
  32.9 0.0 copy-start
  32.9 0.1 slice_reduce_fusion
  33.0 11.8 %all_to_all.16 = f32[8,2,128]{2,1,0:T(2,128)S(1)} all-to-all(f32[8,2,128]{2,1,0:T(2,128)S(1)} %broadcast_in_dim.12), channel_id=1, replica_groups=mesh['panel'=64,'point'=8] {'point'}, dimensions={0} | all-to-all | bytes 16384 | tf_op jit(solution)/shard_map/all_to_all | solution.py:211
  44.8 0.6 broadcast_in_dim.13
  45.4 4.6 %all-to-all-start.2 = ((f32[64,2,128]{2,1,0:T(2,128)}), f32[64,2,128]{2,1,0:T(2,128)S(1)}, u32[]{:S(2)}, u32[]{:S(2)}) async-start(f32[64,2,128]{2,1,0:T(2,128)} %broadcast_in_dim.13), calls=%async_computation.2 | async-start | bytes 131072 | tf_op jit(solution)/shard_map/all_to_all | solution.py:213
  50.1 1.5 %broadcast_in_dim.14.point_ref = f32[3,128,128]{2,1,0:T(8,128)} broadcast(f32[3,128]{1,0:T(4,128)} %param.11), dimensions={0,1} | broadcast | bytes 198144 | tf_op jit(solution)/shard_map/broadcast_in_dim | solution.py:149
  51.6 0.0 copy-done
  51.6 10.9 %shard_map.64 = (f32[64,128,128]{2,1,0:T(8,128)}, f32[64,128,128]{2,1,0:T(8,128)}) custom-call(f32[64,6,128]{2,1,0:T(8,128)} %copy-done, f32[3,128,128]{2,1,0:T(8,128)} %broadcast_in_dim.14.point_ref), custom_call_target="tpu_custom_call" | custom-call | flops 62914560 | bytes 8388608 | tf_op jit(solution)/shard_map/pallas_call | solution.py:152
  62.5 0.0 all-to-all-done.2.velocity_ref
  62.5 5.4 %shard_map.65 = f32[2,128]{1,0:T(2,128)} custom-call(f32[64,2,128]{2,1,0:T(2,128)S(1)} %all-to-all-done.2.velocity_ref, f32[64,1,128]{2,1,0:T(1,128)S(1)} %slice.9.area_ref, f32[64,128,128]{2,1,0:T(8,128)} %get-tuple-element.7.cosine_ref, f32[64,128,128]{2,1,0:T(8,128)} %get-tuple-element.8.sine_ref), custom_call_target="tpu_custom_call" | custom-call | flops 8388608 | bytes 8388608 | tf_op jit(solution)/shard_map/pallas_call | solution.py:167
  (4 shorter events, 0.1 us)
Async XLA Ops:
  32.9 18.6 %copy-start = (f32[64,6,128]{2,1,0:T(8,128)}, f32[64,6,128]{2,1,0:T(8,128)S(1)}, u32[]{:S(2)}) copy-start(f32[64,6,128]{2,1,0:T(8,128)S(1)} %all_to_all.15.panel_ref) | copy-start | bytes 589828
  45.4 17.1 %all-to-all-start.2 = ((f32[64,2,128]{2,1,0:T(2,128)}), f32[64,2,128]{2,1,0:T(2,128)S(1)}, u32[]{:S(2)}, u32[]{:S(2)}) async-start(f32[64,2,128]{2,1,0:T(2,128)} %broadcast_in_dim.13), calls=%async_computation.2 | async-start | bytes 131072 | tf_op jit(solution)/shard_map/all_to_all | solution.py:213

commit v4 on v3

--- a/solution.py
+++ b/solution.py
@@ -89,8 +89,14 @@
     )(panels, spread)
 
 
-def parts_kernel(panel_ref, point_ref, cosine_ref, sine_ref):
+def parts_kernel(panel_ref, coordinate_ref, cosine_ref, sine_ref, point_ref):
     points = point_ref.shape[1]
+
+    @pl.when(pl.program_id(0) == 0)
+    def _():
+        for axis in range(3):
+            row = coordinate_ref[axis:axis + 1, :]
+            point_ref[axis] = jnp.broadcast_to(row, (point_ref.shape[2], points)).T
 
     def body(chunk, carry):
         block = panel_ref[chunk]
@@ -146,7 +152,6 @@
 def kernel_parts(panels, field_points):
     chunks, rows, lanes = panels.shape
     points = field_points.shape[1]
-    spread = jnp.broadcast_to(field_points[:, :, None], (3, points, lanes))
     pairs = chunks * lanes * points
     part = jax.ShapeDtypeStruct((chunks, points, lanes), jnp.float32)
     return pl.pallas_call(
@@ -155,11 +160,13 @@
         grid=(chunks // PARTS_STEP,),
         in_specs=[
             pl.BlockSpec((PARTS_STEP, rows, lanes), lambda c: (c, 0, 0)),
-            pl.BlockSpec((3, points, lanes), lambda c: (0, 0, 0)),
+            pl.BlockSpec(memory_space=pltpu.VMEM),
         ],
         out_specs=[pl.BlockSpec((PARTS_STEP, points, lanes), lambda c: (c, 0, 0))] * 2,
+        scratch_shapes=[pltpu.VMEM((3, points, lanes), jnp.float32)],
+        compiler_params=pltpu.CompilerParams(dimension_semantics=("arbitrary",)),
         cost_estimate=pl.CostEstimate(flops=60 * pairs, transcendentals=2 * pairs, bytes_accessed=8 * pairs),
-    )(panels, spread)
+    )(panels, pltpu.with_memory_space_constraint(field_points, pltpu.VMEM))
 
 
 def contract(velocity, area, cosine_part, sine_part):

time: 68.4 us -> 67.5 us (0.987)
  local copies, waits for them, and re-layouts: 2.24 us -> 1.43 us
    broadcast_in_dim x1 -> x0, local copies, waits for them, and re-layouts: 1.48 us -> none  [kernel_parts(): spread = jnp.broadcast_to(field_points[:, :, None], (3, points, lanes))]
  transfers between devices with their start and end apart: 1 -> 1, of which waited for: 0 -> 0; matrix products, arithmetic and copies ran while one was open for 2% -> 0% of each run, Pallas kernels for 16% -> 16%
where the time goes in v4:
time: 67.5 us; the launch traced here: 67.1 us
  blocking collectives  41.5 us (61%)
  Pallas kernels  16.3 us (24%)
  starting transfers between devices  4.55 us (7%)
  other arithmetic  1.59 us (2%)
  matrix products  1.57 us (2%)
  local copies, waits for them, and re-layouts  1.43 us (2%)
    all_to_all x1, blocking collectives, shards(): lax.all_to_all(outgoing, 'panel', split_axis=0, concat_axis=0, tiled=True)  29.8 us
    all_to_all x1, blocking collectives, shards(): lax.all_to_all(copies, 'point', split_axis=0, concat_axis=0, tiled=True)  11.8 us
    pallas_call x1, Pallas kernels, kernel_parts(): pl.pallas_call(parts_kernel, out_shape=(part, part), grid=(chunks // PART...  10.9 us
    pallas_call x1, Pallas kernels, contract(): pl.pallas_call(contract_kernel, out_shape=jax.ShapeDtypeStruct((2, points...  5.43 us
    all_to_all x1, starting transfers between devices, shards(): lax.all_to_all(spread, 'panel', split_axis=0, concat_axis=0, tiled=True)  4.55 us
    dot_general x1, matrix products, shards(): jnp.dot(weighted, panel_hot, precision=lax.Precision.HIGHEST, preferred_e...  1.57 us
  transfers between devices with their start and end apart: 1, of which 0 were waited for; matrix products, arithmetic and copies ran while one was open for 0% of the time, Pallas kernels for 16%

profile of v4, /device:TPU:1, one launch (start us, length us, event | category | flops | bytes accessed | tf_op | source)
XLA Modules:
  0.0 67.1 jit_solution(16709983800797938716)
XLA Ops:
  0.0 0.7 %fusion.7 = f32[64,2048]{1,0:T(8,128)S(1)} fusion(s32[2048]{0:T(1024)} %bitcast.9), kind=kLoop, calls=%fused_computation.8 | loop fusion | flops 262144 | bytes 532480 | tf_op jit(solution)/shard_map/convert_element_type | solution.py:199
  0.7 1.6 %fusion = f32[2,64,128]{2,1,0:T(8,128)S(1)} fusion(s32[2048]{0:T(1024)} %param.8, f32[64,2048]{1,0:T(8,128)S(1)} %fusion.7, f32[2,2048]{1,0:T(2,128)} %param.6), kind=kOutput, calls=%fused_computation.1 | convolution fusion | flops 403177472 | bytes 614400 | tf_op jit(solution)/shard_map/dot_general | solution.py:206
  2.3 0.1 copy.13
  2.4 0.7 %pad_maximum_fusion.1 = f32[4,128]{1,0:T(4,128)S(1)} fusion(f32[1,128]{1,0:T(1,128)} %bitcast.10, f32[3,128]{1,0:T(4,128)} %param.9), kind=kLoop, calls=%fused_computation.12 | loop fusion | flops 512 | bytes 4096 | tf_op jit(solution)/shard_map/concatenate | solution.py:210
  3.1 0.1 pad_maximum_fusion
  3.2 29.8 %all_to_all.15.panel_ref = f32[64,6,128]{2,1,0:T(8,128)S(1)} all-to-all(f32[64,6,128]{2,1,0:T(8,128)S(1)} %pad_maximum_fusion), channel_id=1, replica_groups=mesh['panel'=64,'point'=8] {'panel'}, dimensions={0} | all-to-all | bytes 393216 | tf_op jit(solution)/shard_map/all_to_all | solution.py:213
  32.9 0.0 copy-start.1
  32.9 0.1 slice_reduce_fusion
  33.0 11.8 %all_to_all.16 = f32[8,2,128]{2,1,0:T(2,128)S(1)} all-to-all(f32[8,2,128]{2,1,0:T(2,128)S(1)} %broadcast_in_dim.10), channel_id=1, replica_groups=mesh['panel'=64,'point'=8] {'point'}, dimensions={0} | all-to-all | bytes 16384 | tf_op jit(solution)/shard_map/all_to_all | solution.py:218
  44.8 0.6 broadcast_in_dim.11
  45.4 4.6 %all-to-all-start.2 = ((f32[64,2,128]{2,1,0:T(2,128)}), f32[64,2,128]{2,1,0:T(2,128)S(1)}, u32[]{:S(2)}, u32[]{:S(2)}) async-start(f32[64,2,128]{2,1,0:T(2,128)} %broadcast_in_dim.11), calls=%async_computation.2 | async-start | bytes 131072 | tf_op jit(solution)/shard_map/all_to_all | solution.py:220
  50.0 0.0 copy-done.1
  50.0 0.0 copy-start
  50.1 0.7 %copy-done = f32[3,128]{1,0:T(4,128)S(1)} copy-done((f32[3,128]{1,0:T(4,128)S(1)}, f32[3,128]{1,0:T(4,128)}, u32[]{:S(2)}) %copy-start) | copy-done | bytes 1560
  50.7 10.9 %shard_map.64 = (f32[64,128,128]{2,1,0:T(8,128)}, f32[64,128,128]{2,1,0:T(8,128)}) custom-call(f32[64,6,128]{2,1,0:T(8,128)} %copy-done.1, f32[3,128]{1,0:T(4,128)S(1)} %copy-done), custom_call_target="tpu_custom_call" | custom-call | flops 62914560 | bytes 8388608 | tf_op jit(solution)/shard_map/pallas_call | solution.py:157
  61.6 0.0 all-to-all-done.2.velocity_ref
  61.6 5.4 %shard_map.65 = f32[2,128]{1,0:T(2,128)} custom-call(f32[64,2,128]{2,1,0:T(2,128)S(1)} %all-to-all-done.2.velocity_ref, f32[64,1,128]{2,1,0:T(1,128)S(1)} %slice.9.area_ref, f32[64,128,128]{2,1,0:T(8,128)} %get-tuple-element.7.cosine_ref, f32[64,128,128]{2,1,0:T(8,128)} %get-tuple-element.8.sine_ref), custom_call_target="tpu_custom_call" | custom-call | flops 8388608 | bytes 8388608 | tf_op jit(solution)/shard_map/pallas_call | solution.py:174
  (4 shorter events, 0.1 us)
Async XLA Ops:
  32.9 17.1 %copy-start.1 = (f32[64,6,128]{2,1,0:T(8,128)}, f32[64,6,128]{2,1,0:T(8,128)S(1)}, u32[]{:S(2)}) copy-start(f32[64,6,128]{2,1,0:T(8,128)S(1)} %all_to_all.15.panel_ref) | copy-start | bytes 589828
  45.4 16.2 %all-to-all-start.2 = ((f32[64,2,128]{2,1,0:T(2,128)}), f32[64,2,128]{2,1,0:T(2,128)S(1)}, u32[]{:S(2)}, u32[]{:S(2)}) async-start(f32[64,2,128]{2,1,0:T(2,128)} %broadcast_in_dim.11), calls=%async_computation.2 | async-start | bytes 131072 | tf_op jit(solution)/shard_map/all_to_all | solution.py:220
  50.0 0.7 %copy-start = (f32[3,128]{1,0:T(4,128)S(1)}, f32[3,128]{1,0:T(4,128)}, u32[]{:S(2)}) copy-start(f32[3,128]{1,0:T(4,128)} %coordinate_ref.1) | copy-start | bytes 4612

commit v5 on v1

--- a/solution.py
+++ b/solution.py
@@ -17,7 +17,7 @@
 HALF_PI_3 = 7.54978995489188216e-8
 GROUP = 16
 PARTS_STEP = 8
-CONTRACT_GROUPS = 8
+STORED_CHUNKS = 48
 
 
 def sine_cosine(angle):
@@ -89,8 +89,12 @@
     )(panels, spread)
 
 
-def parts_kernel(panel_ref, point_ref, cosine_ref, sine_ref):
+def parts_kernel(panel_ref, coordinate_ref, cosine_ref, sine_ref, point_ref):
     points = point_ref.shape[1]
+
+    @pl.when(pl.program_id(0) == 0)
+    def _():
+        point_lanes(coordinate_ref, point_ref)
 
     def body(chunk, carry):
         block = panel_ref[chunk]
@@ -113,46 +117,82 @@
     lax.fori_loop(0, panel_ref.shape[0], body, 0)
 
 
-def contract_kernel(strength_ref, cosine_hbm, sine_hbm, out_ref, cosine_buf, sine_buf, real_ref, imag_ref, sems):
-    chunks = cosine_hbm.shape[0]
-    per_group = chunks // CONTRACT_GROUPS
+def point_lanes(coordinate_ref, point_ref):
+    for axis in range(3):
+        row = coordinate_ref[axis:axis + 1, :]
+        point_ref[axis] = jnp.broadcast_to(row, (point_ref.shape[2], point_ref.shape[1])).T
+
+
+def finish_kernel(velocity_ref, area_ref, panel_ref, coordinate_ref, cosine_hbm, sine_hbm, out_ref,
+                  cosine_buf, sine_buf, point_ref, real_ref, imag_ref, sems):
+    stored = cosine_hbm.shape[0]
+    chunks = panel_ref.shape[0]
+    points = point_ref.shape[1]
+    groups = stored // PARTS_STEP
 
     def copies(group):
-        window = pl.ds(group * per_group, per_group)
+        window = pl.ds(group * PARTS_STEP, PARTS_STEP)
         return (
             pltpu.make_async_copy(cosine_hbm.at[window], cosine_buf.at[window], sems.at[0, group]),
             pltpu.make_async_copy(sine_hbm.at[window], sine_buf.at[window], sems.at[1, group]),
         )
 
-    for group in range(CONTRACT_GROUPS):
+    for group in range(groups):
         for copy in copies(group):
             copy.start()
+    point_lanes(coordinate_ref, point_ref)
     real_ref[...] = jnp.zeros_like(real_ref)
     imag_ref[...] = jnp.zeros_like(imag_ref)
 
-    def body(chunk, carry):
-        block = strength_ref[chunk]
-        shape = real_ref.shape
-        strength_re = jnp.broadcast_to(block[0:1], shape)
-        strength_im = jnp.broadcast_to(block[1:2], shape)
+    def strengths(chunk, shape):
+        velocity = velocity_ref[chunk]
+        area = area_ref[chunk]
+        strength_re = jnp.broadcast_to(-area[0:1] * velocity[1:2], shape)
+        strength_im = jnp.broadcast_to(area[0:1] * velocity[0:1], shape)
+        return strength_re, strength_im
+
+    def fresh(chunk, carry):
+        block = panel_ref[chunk]
+        shape = (GROUP, block.shape[1])
+        strength_re, strength_im = strengths(chunk, shape)
+        centroid_x = jnp.broadcast_to(block[2:3], shape)
+        centroid_y = jnp.broadcast_to(block[3:4], shape)
+        centroid_z = jnp.broadcast_to(block[4:5], shape)
+        for group in range(points // GROUP):
+            rows = pl.ds(group * GROUP, GROUP)
+            delta_x = point_ref[0, rows, :] - centroid_x
+            delta_y = point_ref[1, rows, :] - centroid_y
+            delta_z = point_ref[2, rows, :] - centroid_z
+            distance = jnp.sqrt(delta_x * delta_x + delta_y * delta_y + delta_z * delta_z)
+            inverse = 1.0 / (FOUR_PI * distance)
+            sine, cosine = sine_cosine(WAVENUMBER * distance)
+            cosine_part = cosine * inverse
+            sine_part = sine * inverse
+            real_ref[rows, :] += strength_re * cosine_part - strength_im * sine_part
+            imag_ref[rows, :] += strength_re * sine_part + strength_im * cosine_part
+        return carry
+
+    lax.fori_loop(stored, chunks, fresh, 0)
+
+    def saved(chunk, carry):
+        strength_re, strength_im = strengths(chunk, real_ref.shape)
         cosine_part = cosine_buf[chunk]
         sine_part = sine_buf[chunk]
         real_ref[...] += strength_re * cosine_part - strength_im * sine_part
         imag_ref[...] += strength_re * sine_part + strength_im * cosine_part
         return carry
 
-    for group in range(CONTRACT_GROUPS):
+    for group in range(groups):
         for copy in copies(group):
             copy.wait()
-        lax.fori_loop(group * per_group, (group + 1) * per_group, body, 0)
+        lax.fori_loop(group * PARTS_STEP, (group + 1) * PARTS_STEP, saved, 0)
     out_ref[0:1, :] = jnp.sum(real_ref[...].T, axis=0, keepdims=True)
     out_ref[1:2, :] = jnp.sum(imag_ref[...].T, axis=0, keepdims=True)
 
 
-def kernel_parts(panels, field_points):
-    chunks, rows, lanes = panels.shape
+def kernel_parts(panels, field_points, chunks):
+    rows, lanes = panels.shape[1:]
     points = field_points.shape[1]
-    spread = jnp.broadcast_to(field_points[:, :, None], (3, points, lanes))
     pairs = chunks * lanes * points
     part = jax.ShapeDtypeStruct((chunks, points, lanes), jnp.float32)
     return pl.pallas_call(
@@ -161,29 +201,35 @@
         grid=(chunks // PARTS_STEP,),
         in_specs=[
             pl.BlockSpec((PARTS_STEP, rows, lanes), lambda c: (c, 0, 0)),
-            pl.BlockSpec((3, points, lanes), lambda c: (0, 0, 0)),
+            pl.BlockSpec(memory_space=pltpu.VMEM),
         ],
         out_specs=[pl.BlockSpec((PARTS_STEP, points, lanes), lambda c: (c, 0, 0))] * 2,
+        scratch_shapes=[pltpu.VMEM((3, points, lanes), jnp.float32)],
+        compiler_params=pltpu.CompilerParams(dimension_semantics=("arbitrary",)),
         cost_estimate=pl.CostEstimate(flops=60 * pairs, transcendentals=2 * pairs, bytes_accessed=8 * pairs),
-    )(panels, spread)
-
-
-def contract(strength, cosine_part, sine_part):
-    chunks, points, lanes = cosine_part.shape
+    )(panels, pltpu.with_memory_space_constraint(field_points, pltpu.VMEM))
+
+
+def finish(velocity, area, panels, field_points, cosine_part, sine_part):
+    stored, points, lanes = cosine_part.shape
+    chunks = panels.shape[0]
+    pairs = (chunks - stored) * points * lanes
+    vmem = lambda x: pltpu.with_memory_space_constraint(x, pltpu.VMEM)
     return pl.pallas_call(
-        contract_kernel,
+        finish_kernel,
         out_shape=jax.ShapeDtypeStruct((2, points), jnp.float32),
-        in_specs=[
-            pl.BlockSpec(memory_space=pltpu.VMEM),
-            pl.BlockSpec(memory_space=pl.ANY),
-            pl.BlockSpec(memory_space=pl.ANY),
-        ],
+        in_specs=[pl.BlockSpec(memory_space=pltpu.VMEM)] * 4 + [pl.BlockSpec(memory_space=pl.ANY)] * 2,
         out_specs=pl.BlockSpec(memory_space=pltpu.VMEM),
-        scratch_shapes=[pltpu.VMEM((chunks, points, lanes), jnp.float32)] * 2
+        scratch_shapes=[pltpu.VMEM((stored, points, lanes), jnp.float32)] * 2
+        + [pltpu.VMEM((3, points, lanes), jnp.float32)]
         + [pltpu.VMEM((points, lanes), jnp.float32)] * 2
-        + [pltpu.SemaphoreType.DMA((2, CONTRACT_GROUPS))],
-        cost_estimate=pl.CostEstimate(flops=8 * chunks * points * lanes, transcendentals=0, bytes_accessed=8 * chunks * points * lanes),
-    )(strength, cosine_part, sine_part)
+        + [pltpu.SemaphoreType.DMA((2, stored // PARTS_STEP))],
+        cost_estimate=pl.CostEstimate(
+            flops=70 * pairs + 8 * stored * points * lanes,
+            transcendentals=2 * pairs,
+            bytes_accessed=8 * stored * points * lanes,
+        ),
+    )(vmem(velocity), vmem(area), vmem(panels), vmem(field_points), cosine_part, sine_part)
 
 
 def shards(node_velocity, node_owner, node_panel, panel_centroid, panel_area, field_points):
@@ -201,18 +247,18 @@
         weighted, panel_hot, precision=lax.Precision.HIGHEST, preferred_element_type=jnp.float32
     )
     partial = partial.reshape(2, slab_count, slab_width).transpose(1, 0, 2)
-    centroid_copies = jnp.broadcast_to(panel_centroid[None], (slab_count,) + panel_centroid.shape)
-    outgoing = jnp.concatenate([partial, centroid_copies], axis=1)
+    extra = jnp.concatenate([panel_centroid, panel_area[None]], axis=0)
+    extra_copies = jnp.broadcast_to(extra[None], (slab_count,) + extra.shape)
+    outgoing = jnp.concatenate([partial, extra_copies], axis=1)
     got = lax.all_to_all(outgoing, "panel", split_axis=0, concat_axis=0, tiled=True)
-    cosine_part, sine_part = kernel_parts(got, field_points)
+    cosine_part, sine_part = kernel_parts(got, field_points, STORED_CHUNKS)
     column = jnp.sum(got[:, 0:2], axis=0)
     point_count = lax.axis_size("point")
     copies = jnp.broadcast_to(column[None], (point_count,) + column.shape)
     velocity = jnp.sum(lax.all_to_all(copies, "point", split_axis=0, concat_axis=0, tiled=True), axis=0)
-    strength = jnp.stack([-panel_area * velocity[1], panel_area * velocity[0]])
-    spread = jnp.broadcast_to(strength[None], (slab_count,) + strength.shape)
+    spread = jnp.broadcast_to(velocity[None], (slab_count,) + velocity.shape)
     gathered = lax.all_to_all(spread, "panel", split_axis=0, concat_axis=0, tiled=True)
-    return contract(gathered, cosine_part, sine_part)
+    return finish(gathered, got[:, 5:6], got, field_points, cosine_part, sine_part)
 
 
 def solution(mesh):

time: 69.4 us -> 67.3 us (0.970)
  Pallas kernels: 16.1 us -> 13.3 us
  waiting for transfers between devices: 0.01 us -> 1.76 us
  local copies, waits for them, and re-layouts: 3.52 us -> 2.38 us
    pallas_call x1, Pallas kernels: 10.9 us -> 8.66 us  [kernel_parts(): pl.pallas_call(parts_kernel, out_shape=(part, part), grid=(chunks // PART...]
    broadcast_in_dim x3 -> x2, local copies, waits for them, and re-layouts: 2.83 us -> 0.66 us  [the longest x1 0.64 us: shards(): spread = jnp.broadcast_to(velocity[None], (slab_count,) + velocity.shape)]
    all_to_all x1, waiting for transfers between devices: 0.01 us -> 1.76 us  [shards(): lax.all_to_all(spread, 'panel', split_axis=0, concat_axis=0, tiled=True)]
    unnamed x4 -> x6, local copies, waits for them, and re-layouts: 0.63 us -> 1.63 us
    concatenate x1 -> x2, other arithmetic: 0.06 us -> 0.76 us  [the longest x1 0.71 us: shards(): extra = jnp.concatenate([panel_centroid, panel_area[None]], axis=0)]
  transfers between devices with their start and end apart: 1 -> 1, of which waited for: 0 -> 1; matrix products, arithmetic and copies ran while one was open for 2% -> 0% of each run, Pallas kernels for 16% -> 13%
where the time goes in v5:
time: 67.3 us; the launch traced here: 66.8 us
  blocking collectives  41.5 us (62%)
  Pallas kernels  13.3 us (20%)
  starting transfers between devices  4.6 us (7%)
  local copies, waits for them, and re-layouts  2.38 us (4%)
  waiting for transfers between devices  1.76 us (3%)
  other arithmetic  1.59 us (2%)
  matrix products  1.57 us (2%)
    all_to_all x1, blocking collectives, shards(): lax.all_to_all(outgoing, 'panel', split_axis=0, concat_axis=0, tiled=True)  29.8 us
    all_to_all x1, blocking collectives, shards(): lax.all_to_all(copies, 'point', split_axis=0, concat_axis=0, tiled=True)  11.8 us
    pallas_call x1, Pallas kernels, kernel_parts(): pl.pallas_call(parts_kernel, out_shape=(part, part), grid=(chunks // PART...  8.66 us
    pallas_call x1, Pallas kernels, finish(): pl.pallas_call(finish_kernel, out_shape=jax.ShapeDtypeStruct((2, points),...  4.69 us
    all_to_all x1, starting transfers between devices, shards(): lax.all_to_all(spread, 'panel', split_axis=0, concat_axis=0, tiled=True)  4.6 us
    all_to_all x1, waiting for transfers between devices, shards(): lax.all_to_all(spread, 'panel', split_axis=0, concat_axis=0, tiled=True)  1.76 us
    unnamed x6, local copies, waits for them, and re-layouts  1.63 us
    dot_general x1, matrix products, shards(): jnp.dot(weighted, panel_hot, precision=lax.Precision.HIGHEST, preferred_e...  1.57 us
  transfers between devices with their start and end apart: 1, of which 1 were waited for; matrix products, arithmetic and copies ran while one was open for 0% of the time, Pallas kernels for 13%

profile of v5, /device:TPU:1, one launch (start us, length us, event | category | flops | bytes accessed | tf_op | source)
XLA Modules:
  0.0 66.8 jit_solution(12012840757499517287)
XLA Ops:
  0.0 0.7 %fusion.7 = f32[64,2048]{1,0:T(8,128)S(1)} fusion(s32[2048]{0:T(1024)} %bitcast.9), kind=kLoop, calls=%fused_computation.8 | loop fusion | flops 262144 | bytes 532480 | tf_op jit(solution)/shard_map/convert_element_type | solution.py:239
  0.7 1.6 %fusion = f32[2,64,128]{2,1,0:T(8,128)S(1)} fusion(s32[2048]{0:T(1024)} %param.8, f32[64,2048]{1,0:T(8,128)S(1)} %fusion.7, f32[2,2048]{1,0:T(2,128)} %param.6), kind=kOutput, calls=%fused_computation.1 | convolution fusion | flops 403177472 | bytes 614400 | tf_op jit(solution)/shard_map/dot_general | solution.py:246
  2.3 0.1 copy.13
  2.4 0.7 %pad_maximum_fusion.1 = f32[4,128]{1,0:T(4,128)S(1)} fusion(f32[1,128]{1,0:T(1,128)} %bitcast.10, f32[3,128]{1,0:T(4,128)} %param.9), kind=kLoop, calls=%fused_computation.12 | loop fusion | flops 512 | bytes 4096 | tf_op jit(solution)/shard_map/concatenate | solution.py:250
  3.1 0.1 pad_maximum_fusion
  3.2 29.8 %all_to_all.15.panel_ref = f32[64,6,128]{2,1,0:T(8,128)S(1)} all-to-all(f32[64,6,128]{2,1,0:T(8,128)S(1)} %pad_maximum_fusion), channel_id=1, replica_groups=mesh['panel'=64,'point'=8] {'panel'}, dimensions={0} | all-to-all | bytes 393216 | tf_op jit(solution)/shard_map/all_to_all | solution.py:253
  32.9 0.0 copy-start
  32.9 0.1 slice_reduce_fusion
  33.0 11.8 %all_to_all.16 = f32[8,2,128]{2,1,0:T(2,128)S(1)} all-to-all(f32[8,2,128]{2,1,0:T(2,128)S(1)} %broadcast_in_dim.10), channel_id=1, replica_groups=mesh['panel'=64,'point'=8] {'point'}, dimensions={0} | all-to-all | bytes 16384 | tf_op jit(solution)/shard_map/all_to_all | solution.py:258
  44.8 0.6 broadcast_in_dim.11
  45.4 4.6 %all-to-all-start.2 = ((f32[64,2,128]{2,1,0:T(2,128)}), f32[64,2,128]{2,1,0:T(2,128)S(1)}, u32[]{:S(2)}, u32[]{:S(2)}) async-start(f32[64,2,128]{2,1,0:T(2,128)} %broadcast_in_dim.11), calls=%async_computation.2 | async-start | bytes 131072 | tf_op jit(solution)/shard_map/all_to_all | solution.py:260
  50.1 0.0 copy-done
  50.1 0.0 copy-start.2
  50.1 0.7 %copy-done.2 = f32[3,128]{1,0:T(4,128)S(1)} copy-done((f32[3,128]{1,0:T(4,128)S(1)}, f32[3,128]{1,0:T(4,128)}, u32[]{:S(2)}) %copy-start.2) | copy-done | bytes 1560
  50.8 8.7 %shard_map.64 = (f32[48,128,128]{2,1,0:T(8,128)}, f32[48,128,128]{2,1,0:T(8,128)}) custom-call(f32[64,6,128]{2,1,0:T(8,128)} %copy-done, f32[3,128]{1,0:T(4,128)S(1)} %copy-done.2), custom_call_target="tpu_custom_call" | custom-call | flops 47185920 | bytes 6291456 | tf_op jit(solution)/shard_map/pallas_call | solution.py:198
  59.4 1.8 %all-to-all-done.2.velocity_ref = f32[64,2,128]{2,1,0:T(2,128)S(1)} async-done(((f32[64,2,128]{2,1,0:T(2,128)}), f32[64,2,128]{2,1,0:T(2,128)S(1)}, u32[]{:S(2)}, u32[]{:S(2)}) %all-to-all-start.2) | async-done | bytes 65568 | tf_op jit(solution)/shard_map/all_to_all | solution.py:260
  61.2 0.0 copy-start.1
  61.2 0.9 %copy-done.1 = f32[64,6,128]{2,1,0:T(8,128)S(1)} copy-done((f32[64,6,128]{2,1,0:T(8,128)S(1)}, f32[64,6,128]{2,1,0:T(8,128)}, u32[]{:S(2)}) %copy-start.1) | copy-done | bytes 196632
  62.2 4.7 %shard_map.65 = f32[2,128]{1,0:T(2,128)} custom-call(f32[64,2,128]{2,1,0:T(2,128)S(1)} %all-to-all-done.2.velocity_ref, f32[64,1,128]{2,1,0:T(1,128)S(1)} %slice.9.area_ref, f32[64,6,128]{2,1,0:T(8,128)S(1)} %copy-done.1, f32[3,128]{1,0:T(4,128)S(1)} %copy-done.2, f32[48,128,128]{2,1,0:T(8,128)} %get-tuple-element.7.cosine_hbm, ...), custom_call_target="tpu_custom_call" | custom-call | flops 24641536 | bytes 6291456 | tf_op jit(solution)/shard_map/pallas_call | solution.py:218
  (4 shorter events, 0.1 us)
Async XLA Ops:
  32.9 17.1 %copy-start = (f32[64,6,128]{2,1,0:T(8,128)}, f32[64,6,128]{2,1,0:T(8,128)S(1)}, u32[]{:S(2)}) copy-start(f32[64,6,128]{2,1,0:T(8,128)S(1)} %all_to_all.15.panel_ref) | copy-start | bytes 589828
  45.4 15.8 %all-to-all-start.2 = ((f32[64,2,128]{2,1,0:T(2,128)}), f32[64,2,128]{2,1,0:T(2,128)S(1)}, u32[]{:S(2)}, u32[]{:S(2)}) async-start(f32[64,2,128]{2,1,0:T(2,128)} %broadcast_in_dim.11), calls=%async_computation.2 | async-start | bytes 131072 | tf_op jit(solution)/shard_map/all_to_all | solution.py:260
  50.1 0.7 %copy-start.2 = (f32[3,128]{1,0:T(4,128)S(1)}, f32[3,128]{1,0:T(4,128)}, u32[]{:S(2)}) copy-start(f32[3,128]{1,0:T(4,128)} %coordinate_ref.3) | copy-start | bytes 4612
  61.2 1.0 %copy-start.1 = (f32[64,6,128]{2,1,0:T(8,128)S(1)}, f32[64,6,128]{2,1,0:T(8,128)}, u32[]{:S(2)}) copy-start(f32[64,6,128]{2,1,0:T(8,128)} %copy-done) | copy-start | bytes 589828

commit v6 on v5

--- a/solution.py
+++ b/solution.py
@@ -96,8 +96,10 @@
     def _():
         point_lanes(coordinate_ref, point_ref)
 
+    first = pl.program_id(0) * cosine_ref.shape[0]
+
     def body(chunk, carry):
-        block = panel_ref[chunk]
+        block = panel_ref[first + chunk]
         shape = (GROUP, block.shape[1])
         centroid_x = jnp.broadcast_to(block[2:3], shape)
         centroid_y = jnp.broadcast_to(block[3:4], shape)
@@ -114,7 +116,7 @@
             sine_ref[chunk, rows, :] = sine * inverse
         return carry
 
-    lax.fori_loop(0, panel_ref.shape[0], body, 0)
+    lax.fori_loop(0, cosine_ref.shape[0], body, 0)
 
 
 def point_lanes(coordinate_ref, point_ref):
@@ -199,15 +201,15 @@
         parts_kernel,
         out_shape=(part, part),
         grid=(chunks // PARTS_STEP,),
-        in_specs=[
-            pl.BlockSpec((PARTS_STEP, rows, lanes), lambda c: (c, 0, 0)),
-            pl.BlockSpec(memory_space=pltpu.VMEM),
-        ],
+        in_specs=[pl.BlockSpec(memory_space=pltpu.VMEM)] * 2,
         out_specs=[pl.BlockSpec((PARTS_STEP, points, lanes), lambda c: (c, 0, 0))] * 2,
         scratch_shapes=[pltpu.VMEM((3, points, lanes), jnp.float32)],
         compiler_params=pltpu.CompilerParams(dimension_semantics=("arbitrary",)),
         cost_estimate=pl.CostEstimate(flops=60 * pairs, transcendentals=2 * pairs, bytes_accessed=8 * pairs),
-    )(panels, pltpu.with_memory_space_constraint(field_points, pltpu.VMEM))
+    )(
+        pltpu.with_memory_space_constraint(panels, pltpu.VMEM),
+        pltpu.with_memory_space_constraint(field_points, pltpu.VMEM),
+    )
 
 
 def finish(velocity, area, panels, field_points, cosine_part, sine_part):

time: 67.3 us -> 66.3 us (0.985)
  local copies, waits for them, and re-layouts: 2.38 us -> 1.43 us
  waiting for transfers between devices: 1.76 us -> 2.56 us
  Pallas kernels: 13.3 us -> 12.6 us
    unnamed x6 -> x2, local copies, waits for them, and re-layouts: 1.63 us -> 0.68 us
    all_to_all x1, waiting for transfers between devices: 1.76 us -> 2.56 us  [shards(): lax.all_to_all(spread, 'panel', split_axis=0, concat_axis=0, tiled=True)]
    pallas_call x1, Pallas kernels: 8.66 us -> 7.87 us  [kernel_parts(): pl.pallas_call(parts_kernel, out_shape=(part, part), grid=(chunks // PART...]
  transfers between devices with their start and end apart: 1 -> 1, of which waited for: 1 -> 1; matrix products, arithmetic and copies ran while one was open for 0% -> 0% of each run, Pallas kernels for 13% -> 12%
where the time goes in v6:
time: 66.3 us; the launch traced here: 65.8 us
  blocking collectives  41.5 us (63%)
  Pallas kernels  12.6 us (19%)
  starting transfers between devices  4.54 us (7%)
  waiting for transfers between devices  2.56 us (4%)
  other arithmetic  1.59 us (2%)
  matrix products  1.57 us (2%)
  local copies, waits for them, and re-layouts  1.43 us (2%)
    all_to_all x1, blocking collectives, shards(): lax.all_to_all(outgoing, 'panel', split_axis=0, concat_axis=0, tiled=True)  29.8 us
    all_to_all x1, blocking collectives, shards(): lax.all_to_all(copies, 'point', split_axis=0, concat_axis=0, tiled=True)  11.8 us
    pallas_call x1, Pallas kernels, kernel_parts(): pl.pallas_call(parts_kernel, out_shape=(part, part), grid=(chunks // PART...  7.87 us
    pallas_call x1, Pallas kernels, finish(): pl.pallas_call(finish_kernel, out_shape=jax.ShapeDtypeStruct((2, points),...  4.69 us
    all_to_all x1, starting transfers between devices, shards(): lax.all_to_all(spread, 'panel', split_axis=0, concat_axis=0, tiled=True)  4.54 us
    all_to_all x1, waiting for transfers between devices, shards(): lax.all_to_all(spread, 'panel', split_axis=0, concat_axis=0, tiled=True)  2.56 us
    dot_general x1, matrix products, shards(): jnp.dot(weighted, panel_hot, precision=lax.Precision.HIGHEST, preferred_e...  1.57 us
  transfers between devices with their start and end apart: 1, of which 1 were waited for; matrix products, arithmetic and copies ran while one was open for 0% of the time, Pallas kernels for 12%

profile of v6, /device:TPU:1, one launch (start us, length us, event | category | flops | bytes accessed | tf_op | source)
XLA Modules:
  0.0 65.8 jit_solution(2271010059041758827)
XLA Ops:
  0.0 0.7 %fusion.7 = f32[64,2048]{1,0:T(8,128)S(1)} fusion(s32[2048]{0:T(1024)} %bitcast.9), kind=kLoop, calls=%fused_computation.8 | loop fusion | flops 262144 | bytes 532480 | tf_op jit(solution)/shard_map/convert_element_type | solution.py:241
  0.7 1.6 %fusion = f32[2,64,128]{2,1,0:T(8,128)S(1)} fusion(s32[2048]{0:T(1024)} %param.8, f32[64,2048]{1,0:T(8,128)S(1)} %fusion.7, f32[2,2048]{1,0:T(2,128)} %param.6), kind=kOutput, calls=%fused_computation.1 | convolution fusion | flops 403177472 | bytes 614400 | tf_op jit(solution)/shard_map/dot_general | solution.py:248
  2.3 0.1 copy.13
  2.4 0.7 %pad_maximum_fusion.1 = f32[4,128]{1,0:T(4,128)S(1)} fusion(f32[1,128]{1,0:T(1,128)} %bitcast.10, f32[3,128]{1,0:T(4,128)} %param.9), kind=kLoop, calls=%fused_computation.12 | loop fusion | flops 512 | bytes 4096 | tf_op jit(solution)/shard_map/concatenate | solution.py:252
  3.1 0.1 pad_maximum_fusion
  3.2 29.8 %all_to_all.15.panel_ref = f32[64,6,128]{2,1,0:T(8,128)S(1)} all-to-all(f32[64,6,128]{2,1,0:T(8,128)S(1)} %pad_maximum_fusion), channel_id=1, replica_groups=mesh['panel'=64,'point'=8] {'panel'}, dimensions={0} | all-to-all | bytes 393216 | tf_op jit(solution)/shard_map/all_to_all | solution.py:255
  32.9 0.1 slice_reduce_fusion
  33.0 11.8 %all_to_all.16 = f32[8,2,128]{2,1,0:T(2,128)S(1)} all-to-all(f32[8,2,128]{2,1,0:T(2,128)S(1)} %broadcast_in_dim.10), channel_id=1, replica_groups=mesh['panel'=64,'point'=8] {'point'}, dimensions={0} | all-to-all | bytes 16384 | tf_op jit(solution)/shard_map/all_to_all | solution.py:260
  44.8 0.6 broadcast_in_dim.11
  45.4 4.5 %all-to-all-start.2 = ((f32[64,2,128]{2,1,0:T(2,128)}), f32[64,2,128]{2,1,0:T(2,128)S(1)}, u32[]{:S(2)}, u32[]{:S(2)}) async-start(f32[64,2,128]{2,1,0:T(2,128)} %broadcast_in_dim.11), calls=%async_computation.2 | async-start | bytes 131072 | tf_op jit(solution)/shard_map/all_to_all | solution.py:262
  50.0 0.0 copy-start
  50.0 0.7 %copy-done = f32[3,128]{1,0:T(4,128)S(1)} copy-done((f32[3,128]{1,0:T(4,128)S(1)}, f32[3,128]{1,0:T(4,128)}, u32[]{:S(2)}) %copy-start) | copy-done | bytes 1560
  50.7 7.9 %shard_map.64 = (f32[48,128,128]{2,1,0:T(8,128)}, f32[48,128,128]{2,1,0:T(8,128)}) custom-call(f32[64,6,128]{2,1,0:T(8,128)S(1)} %all_to_all.15.panel_ref, f32[3,128]{1,0:T(4,128)S(1)} %copy-done), custom_call_target="tpu_custom_call" | custom-call | flops 47185920 | bytes 6291456 | tf_op jit(solution)/shard_map/pallas_call | solution.py:200
  58.6 2.6 %all-to-all-done.2.velocity_ref = f32[64,2,128]{2,1,0:T(2,128)S(1)} async-done(((f32[64,2,128]{2,1,0:T(2,128)}), f32[64,2,128]{2,1,0:T(2,128)S(1)}, u32[]{:S(2)}, u32[]{:S(2)}) %all-to-all-start.2) | async-done | bytes 65568 | tf_op jit(solution)/shard_map/all_to_all | solution.py:262
  61.1 4.7 %shard_map.65 = f32[2,128]{1,0:T(2,128)} custom-call(f32[64,2,128]{2,1,0:T(2,128)S(1)} %all-to-all-done.2.velocity_ref, f32[64,1,128]{2,1,0:T(1,128)S(1)} %slice.9.area_ref, f32[64,6,128]{2,1,0:T(8,128)S(1)} %all_to_all.15.panel_ref, f32[3,128]{1,0:T(4,128)S(1)} %copy-done, f32[48,128,128]{2,1,0:T(8,128)} %get-tuple-element.7.cosine_hbm, ...), custom_call_target="tpu_custom_call" | custom-call | flops 24641536 | bytes 6291456 | tf_op jit(solution)/shard_map/pallas_call | solution.py:220
  (4 shorter events, 0.1 us)
Async XLA Ops:
  45.4 15.7 %all-to-all-start.2 = ((f32[64,2,128]{2,1,0:T(2,128)}), f32[64,2,128]{2,1,0:T(2,128)S(1)}, u32[]{:S(2)}, u32[]{:S(2)}) async-start(f32[64,2,128]{2,1,0:T(2,128)} %broadcast_in_dim.11), calls=%async_computation.2 | async-start | bytes 131072 | tf_op jit(solution)/shard_map/all_to_all | solution.py:262
  50.0 0.7 %copy-start = (f32[3,128]{1,0:T(4,128)S(1)}, f32[3,128]{1,0:T(4,128)}, u32[]{:S(2)}) copy-start(f32[3,128]{1,0:T(4,128)} %coordinate_ref.3) | copy-start | bytes 4612

commit v7 on v6

--- a/solution.py
+++ b/solution.py
@@ -1,3 +1,4 @@
+import functools
 import math
 
 import jax
@@ -17,7 +18,8 @@
 HALF_PI_3 = 7.54978995489188216e-8
 GROUP = 16
 PARTS_STEP = 8
-STORED_CHUNKS = 48
+NEAR_CHUNKS = 8
+FAR_CHUNKS = 48
 
 
 def sine_cosine(angle):
@@ -89,14 +91,14 @@
     )(panels, spread)
 
 
-def parts_kernel(panel_ref, coordinate_ref, cosine_ref, sine_ref, point_ref):
+def parts_kernel(offset, panel_ref, coordinate_ref, cosine_ref, sine_ref, point_ref):
     points = point_ref.shape[1]
 
     @pl.when(pl.program_id(0) == 0)
     def _():
         point_lanes(coordinate_ref, point_ref)
 
-    first = pl.program_id(0) * cosine_ref.shape[0]
+    first = offset + pl.program_id(0) * cosine_ref.shape[0]
 
     def body(chunk, carry):
         block = panel_ref[first + chunk]
@@ -125,12 +127,13 @@
         point_ref[axis] = jnp.broadcast_to(row, (point_ref.shape[2], point_ref.shape[1])).T
 
 
-def finish_kernel(velocity_ref, area_ref, panel_ref, coordinate_ref, cosine_hbm, sine_hbm, out_ref,
-                  cosine_buf, sine_buf, point_ref, real_ref, imag_ref, sems):
-    stored = cosine_hbm.shape[0]
+def finish_kernel(velocity_ref, area_ref, panel_ref, coordinate_ref, cosine_near, sine_near, cosine_hbm, sine_hbm,
+                  out_ref, cosine_buf, sine_buf, point_ref, real_ref, imag_ref, sems):
+    near = cosine_near.shape[0]
+    far = cosine_hbm.shape[0]
     chunks = panel_ref.shape[0]
     points = point_ref.shape[1]
-    groups = stored // PARTS_STEP
+    groups = far // PARTS_STEP
 
     def copies(group):
         window = pl.ds(group * PARTS_STEP, PARTS_STEP)
@@ -174,31 +177,36 @@
             imag_ref[rows, :] += strength_re * sine_part + strength_im * cosine_part
         return carry
 
-    lax.fori_loop(stored, chunks, fresh, 0)
-
-    def saved(chunk, carry):
-        strength_re, strength_im = strengths(chunk, real_ref.shape)
-        cosine_part = cosine_buf[chunk]
-        sine_part = sine_buf[chunk]
-        real_ref[...] += strength_re * cosine_part - strength_im * sine_part
-        imag_ref[...] += strength_re * sine_part + strength_im * cosine_part
-        return carry
-
+    lax.fori_loop(near + far, chunks, fresh, 0)
+
+    def saved(cosine_src, sine_src, base):
+        def body(chunk, carry):
+            strength_re, strength_im = strengths(chunk, real_ref.shape)
+            cosine_part = cosine_src[chunk - base]
+            sine_part = sine_src[chunk - base]
+            real_ref[...] += strength_re * cosine_part - strength_im * sine_part
+            imag_ref[...] += strength_re * sine_part + strength_im * cosine_part
+            return carry
+
+        return body
+
+    lax.fori_loop(0, near, saved(cosine_near, sine_near, 0), 0)
     for group in range(groups):
         for copy in copies(group):
             copy.wait()
-        lax.fori_loop(group * PARTS_STEP, (group + 1) * PARTS_STEP, saved, 0)
+        start = near + group * PARTS_STEP
+        lax.fori_loop(start, start + PARTS_STEP, saved(cosine_buf, sine_buf, near), 0)
     out_ref[0:1, :] = jnp.sum(real_ref[...].T, axis=0, keepdims=True)
     out_ref[1:2, :] = jnp.sum(imag_ref[...].T, axis=0, keepdims=True)
 
 
-def kernel_parts(panels, field_points, chunks):
+def kernel_parts(panels, field_points, offset, chunks):
     rows, lanes = panels.shape[1:]
     points = field_points.shape[1]
     pairs = chunks * lanes * points
     part = jax.ShapeDtypeStruct((chunks, points, lanes), jnp.float32)
     return pl.pallas_call(
-        parts_kernel,
+        functools.partial(parts_kernel, offset),
         out_shape=(part, part),
         grid=(chunks // PARTS_STEP,),
         in_specs=[pl.BlockSpec(memory_space=pltpu.VMEM)] * 2,
@@ -212,26 +220,31 @@
     )
 
 
-def finish(velocity, area, panels, field_points, cosine_part, sine_part):
-    stored, points, lanes = cosine_part.shape
+def finish(velocity, area, panels, field_points, near_parts, far_parts):
+    (cosine_near, sine_near), (cosine_far, sine_far) = near_parts, far_parts
+    far, points, lanes = cosine_far.shape
     chunks = panels.shape[0]
+    stored = far + cosine_near.shape[0]
     pairs = (chunks - stored) * points * lanes
     vmem = lambda x: pltpu.with_memory_space_constraint(x, pltpu.VMEM)
     return pl.pallas_call(
         finish_kernel,
         out_shape=jax.ShapeDtypeStruct((2, points), jnp.float32),
-        in_specs=[pl.BlockSpec(memory_space=pltpu.VMEM)] * 4 + [pl.BlockSpec(memory_space=pl.ANY)] * 2,
+        in_specs=[pl.BlockSpec(memory_space=pltpu.VMEM)] * 6 + [pl.BlockSpec(memory_space=pl.ANY)] * 2,
         out_specs=pl.BlockSpec(memory_space=pltpu.VMEM),
-        scratch_shapes=[pltpu.VMEM((stored, points, lanes), jnp.float32)] * 2
+        scratch_shapes=[pltpu.VMEM((far, points, lanes), jnp.float32)] * 2
         + [pltpu.VMEM((3, points, lanes), jnp.float32)]
         + [pltpu.VMEM((points, lanes), jnp.float32)] * 2
-        + [pltpu.SemaphoreType.DMA((2, stored // PARTS_STEP))],
+        + [pltpu.SemaphoreType.DMA((2, far // PARTS_STEP))],
         cost_estimate=pl.CostEstimate(
             flops=70 * pairs + 8 * stored * points * lanes,
             transcendentals=2 * pairs,
-            bytes_accessed=8 * stored * points * lanes,
+            bytes_accessed=8 * far * points * lanes,
         ),
-    )(vmem(velocity), vmem(area), vmem(panels), vmem(field_points), cosine_part, sine_part)
+    )(
+        vmem(velocity), vmem(area), vmem(panels), vmem(field_points),
+        vmem(cosine_near), vmem(sine_near), cosine_far, sine_far,
+    )
 
 
 def shards(node_velocity, node_owner, node_panel, panel_centroid, panel_area, field_points):
@@ -253,14 +266,15 @@
     extra_copies = jnp.broadcast_to(extra[None], (slab_count,) + extra.shape)
     outgoing = jnp.concatenate([partial, extra_copies], axis=1)
     got = lax.all_to_all(outgoing, "panel", split_axis=0, concat_axis=0, tiled=True)
-    cosine_part, sine_part = kernel_parts(got, field_points, STORED_CHUNKS)
+    near_parts = kernel_parts(got, field_points, 0, NEAR_CHUNKS)
+    far_parts = kernel_parts(got, field_points, NEAR_CHUNKS, FAR_CHUNKS)
     column = jnp.sum(got[:, 0:2], axis=0)
     point_count = lax.axis_size("point")
     copies = jnp.broadcast_to(column[None], (point_count,) + column.shape)
     velocity = jnp.sum(lax.all_to_all(copies, "point", split_axis=0, concat_axis=0, tiled=True), axis=0)
     spread = jnp.broadcast_to(velocity[None], (slab_count,) + velocity.shape)
     gathered = lax.all_to_all(spread, "panel", split_axis=0, concat_axis=0, tiled=True)
-    return finish(gathered, got[:, 5:6], got, field_points, cosine_part, sine_part)
+    return finish(gathered, got[:, 5:6], got, field_points, near_parts, far_parts)
 
 
 def solution(mesh):

time: 66.3 us -> 65.4 us (0.986)
  waiting for transfers between devices: 2.56 us -> 0.27 us
  Pallas kernels: 12.6 us -> 13.9 us
    all_to_all x1, waiting for transfers between devices: 2.56 us -> 0.27 us  [shards(): lax.all_to_all(spread, 'panel', split_axis=0, concat_axis=0, tiled=True)]
    pallas_call x1 -> x2, Pallas kernels: 7.87 us -> 10.1 us  [kernel_parts(): pl.pallas_call(functools.partial(parts_kernel, offset), out_shape=(part,...]
    pallas_call x1, Pallas kernels: 4.69 us -> 3.75 us  [finish(): pl.pallas_call(finish_kernel, out_shape=jax.ShapeDtypeStruct((2, points),...]
  transfers between devices with their start and end apart: 1 -> 1, of which waited for: 1 -> 1; matrix products, arithmetic and copies ran while one was open for 0% -> 0% of each run, Pallas kernels for 12% -> 16%
where the time goes in v7:
time: 65.4 us; the launch traced here: 65 us
  blocking collectives  41.5 us (63%)
  Pallas kernels  13.9 us (21%)
  starting transfers between devices  4.6 us (7%)
  other arithmetic  1.59 us (2%)
  matrix products  1.57 us (2%)
  local copies, waits for them, and re-layouts  1.44 us (2%)
    all_to_all x1, blocking collectives, shards(): lax.all_to_all(outgoing, 'panel', split_axis=0, concat_axis=0, tiled=True)  29.8 us
    all_to_all x1, blocking collectives, shards(): lax.all_to_all(copies, 'point', split_axis=0, concat_axis=0, tiled=True)  11.8 us
    pallas_call x2, Pallas kernels, kernel_parts(): pl.pallas_call(functools.partial(parts_kernel, offset), out_shape=(part,...  10.1 us
    all_to_all x1, starting transfers between devices, shards(): lax.all_to_all(spread, 'panel', split_axis=0, concat_axis=0, tiled=True)  4.6 us
    pallas_call x1, Pallas kernels, finish(): pl.pallas_call(finish_kernel, out_shape=jax.ShapeDtypeStruct((2, points),...  3.75 us
    dot_general x1, matrix products, shards(): jnp.dot(weighted, panel_hot, precision=lax.Precision.HIGHEST, preferred_e...  1.57 us
  transfers between devices with their start and end apart: 1, of which 1 were waited for; matrix products, arithmetic and copies ran while one was open for 0% of the time, Pallas kernels for 16%

profile of v7, /device:TPU:1, one launch (start us, length us, event | category | flops | bytes accessed | tf_op | source)
XLA Modules:
  0.0 65.0 jit_solution(3796254821250900693)
XLA Ops:
  0.0 0.7 %fusion.7 = f32[64,2048]{1,0:T(8,128)S(1)} fusion(s32[2048]{0:T(1024)} %bitcast.9), kind=kLoop, calls=%fused_computation.8 | loop fusion | flops 262144 | bytes 532480 | tf_op jit(solution)/shard_map/convert_element_type | solution.py:254
  0.7 1.6 %fusion = f32[2,64,128]{2,1,0:T(8,128)S(1)} fusion(s32[2048]{0:T(1024)} %param.8, f32[64,2048]{1,0:T(8,128)S(1)} %fusion.7, f32[2,2048]{1,0:T(2,128)} %param.6), kind=kOutput, calls=%fused_computation.1 | convolution fusion | flops 403177472 | bytes 614400 | tf_op jit(solution)/shard_map/dot_general | solution.py:261
  2.3 0.1 copy.13
  2.4 0.7 %pad_maximum_fusion.1 = f32[4,128]{1,0:T(4,128)S(1)} fusion(f32[1,128]{1,0:T(1,128)} %bitcast.10, f32[3,128]{1,0:T(4,128)} %param.9), kind=kLoop, calls=%fused_computation.12 | loop fusion | flops 512 | bytes 4096 | tf_op jit(solution)/shard_map/concatenate | solution.py:265
  3.1 0.1 pad_maximum_fusion
  3.2 29.8 %all_to_all.15.panel_ref = f32[64,6,128]{2,1,0:T(8,128)S(1)} all-to-all(f32[64,6,128]{2,1,0:T(8,128)S(1)} %pad_maximum_fusion), channel_id=1, replica_groups=mesh['panel'=64,'point'=8] {'panel'}, dimensions={0} | all-to-all | bytes 393216 | tf_op jit(solution)/shard_map/all_to_all | solution.py:268
  32.9 0.1 slice_reduce_fusion
  33.0 11.8 %all_to_all.16 = f32[8,2,128]{2,1,0:T(2,128)S(1)} all-to-all(f32[8,2,128]{2,1,0:T(2,128)S(1)} %broadcast_in_dim.10), channel_id=1, replica_groups=mesh['panel'=64,'point'=8] {'point'}, dimensions={0} | all-to-all | bytes 16384 | tf_op jit(solution)/shard_map/all_to_all | solution.py:274
  44.8 0.6 broadcast_in_dim.11
  45.4 4.6 %all-to-all-start.2 = ((f32[64,2,128]{2,1,0:T(2,128)}), f32[64,2,128]{2,1,0:T(2,128)S(1)}, u32[]{:S(2)}, u32[]{:S(2)}) async-start(f32[64,2,128]{2,1,0:T(2,128)} %broadcast_in_dim.11), calls=%async_computation.2 | async-start | bytes 131072 | tf_op jit(solution)/shard_map/all_to_all | solution.py:276
  50.1 0.0 copy-start.2
  50.1 0.7 %copy-done.2 = f32[3,128]{1,0:T(4,128)S(1)} copy-done((f32[3,128]{1,0:T(4,128)S(1)}, f32[3,128]{1,0:T(4,128)}, u32[]{:S(2)}) %copy-start.2) | copy-done | bytes 1560
  50.8 2.2 %shard_map.64 = (f32[8,128,128]{2,1,0:T(8,128)}, f32[8,128,128]{2,1,0:T(8,128)}) custom-call(f32[64,6,128]{2,1,0:T(8,128)S(1)} %all_to_all.15.panel_ref, f32[3,128]{1,0:T(4,128)S(1)} %copy-done.2), custom_call_target="tpu_custom_call" | custom-call | flops 7864320 | bytes 1048576 | tf_op jit(solution)/shard_map/pallas_call | solution.py:208
  53.0 0.0 copy-start
  53.0 0.0 copy-start.1
  53.0 7.9 %shard_map.65 = (f32[48,128,128]{2,1,0:T(8,128)}, f32[48,128,128]{2,1,0:T(8,128)}) custom-call(f32[64,6,128]{2,1,0:T(8,128)S(1)} %all_to_all.15.panel_ref, f32[3,128]{1,0:T(4,128)S(1)} %copy-done.2), custom_call_target="tpu_custom_call" | custom-call | flops 47185920 | bytes 6291456 | tf_op jit(solution)/shard_map/pallas_call | solution.py:208
  60.9 0.3 all-to-all-done.2.velocity_ref
  61.2 0.0 copy-done
  61.2 0.0 copy-done.1
  61.2 3.8 %shard_map.66 = f32[2,128]{1,0:T(2,128)} custom-call(f32[64,2,128]{2,1,0:T(2,128)S(1)} %all-to-all-done.2.velocity_ref, f32[64,1,128]{2,1,0:T(1,128)S(1)} %slice.9.area_ref, f32[64,6,128]{2,1,0:T(8,128)S(1)} %all_to_all.15.panel_ref, f32[3,128]{1,0:T(4,128)S(1)} %copy-done.2, f32[8,128,128]{2,1,0:T(8,128)S(1)} %copy-done, f32[8,128,128]{2,1,0:T(8,128)S(1)} %copy-done.1, ...), custom_call_target="tpu_custom_call" | custom-call | flops 16515072 | bytes 6291456 | tf_op jit(solution)/shard_map/pallas_call | solution.py:230
  (4 shorter events, 0.1 us)
Async XLA Ops:
  45.4 15.8 %all-to-all-start.2 = ((f32[64,2,128]{2,1,0:T(2,128)}), f32[64,2,128]{2,1,0:T(2,128)S(1)}, u32[]{:S(2)}, u32[]{:S(2)}) async-start(f32[64,2,128]{2,1,0:T(2,128)} %broadcast_in_dim.11), calls=%async_computation.2 | async-start | bytes 131072 | tf_op jit(solution)/shard_map/all_to_all | solution.py:276
  50.1 0.7 %copy-start.2 = (f32[3,128]{1,0:T(4,128)S(1)}, f32[3,128]{1,0:T(4,128)}, u32[]{:S(2)}) copy-start(f32[3,128]{1,0:T(4,128)} %coordinate_ref.5) | copy-start | bytes 4612
  53.0 8.2 %copy-start = (f32[8,128,128]{2,1,0:T(8,128)S(1)}, f32[8,128,128]{2,1,0:T(8,128)}, u32[]{:S(2)}) copy-start(f32[8,128,128]{2,1,0:T(8,128)} %get-tuple-element.9.cosine_near) | copy-start | bytes 1572868
  53.0 8.2 %copy-start.1 = (f32[8,128,128]{2,1,0:T(8,128)S(1)}, f32[8,128,128]{2,1,0:T(8,128)}, u32[]{:S(2)}) copy-start(f32[8,128,128]{2,1,0:T(8,128)} %get-tuple-element.10.sine_near) | copy-start | bytes 1572868

commit v8 on v7

--- a/solution.py
+++ b/solution.py
@@ -18,8 +18,8 @@
 HALF_PI_3 = 7.54978995489188216e-8
 GROUP = 16
 PARTS_STEP = 8
-NEAR_CHUNKS = 8
-FAR_CHUNKS = 48
+NEAR_CHUNKS = 16
+FAR_CHUNKS = 40
 
 
 def sine_cosine(angle):

time: 65.4 us -> 65.3 us (level)
  local copies, waits for them, and re-layouts: 1.44 us -> 0.77 us
    unnamed x6, local copies, waits for them, and re-layouts: 0.68 us -> 0.01 us
where the time goes in v8:
time: 65.3 us; the launch traced here: 64.8 us
  blocking collectives  41.5 us (64%)
  Pallas kernels  13.8 us (21%)
  starting transfers between devices  4.6 us (7%)
  other arithmetic  1.61 us (2%)
  matrix products  1.57 us (2%)
  waiting for transfers between devices  0.89 us (1%)
  local copies, waits for them, and re-layouts  0.77 us (1%)
    all_to_all x1, blocking collectives, shards(): lax.all_to_all(outgoing, 'panel', split_axis=0, concat_axis=0, tiled=True)  29.8 us
    all_to_all x1, blocking collectives, shards(): lax.all_to_all(copies, 'point', split_axis=0, concat_axis=0, tiled=True)  11.8 us
    pallas_call x2, Pallas kernels, kernel_parts(): pl.pallas_call(functools.partial(parts_kernel, offset), out_shape=(part,...  10.2 us
    all_to_all x1, starting transfers between devices, shards(): lax.all_to_all(spread, 'panel', split_axis=0, concat_axis=0, tiled=True)  4.6 us
    pallas_call x1, Pallas kernels, finish(): pl.pallas_call(finish_kernel, out_shape=jax.ShapeDtypeStruct((2, points),...  3.59 us
    dot_general x1, matrix products, shards(): jnp.dot(weighted, panel_hot, precision=lax.Precision.HIGHEST, preferred_e...  1.57 us
  transfers between devices with their start and end apart: 1, of which 1 were waited for; matrix products, arithmetic and copies ran while one was open for 0% of the time, Pallas kernels for 16%

profile of v8, /device:TPU:1, one launch (start us, length us, event | category | flops | bytes accessed | tf_op | source)
XLA Modules:
  0.0 64.8 jit_solution(13772802541790055616)
XLA Ops:
  0.0 0.0 copy-start.2
  0.0 0.7 %fusion.7 = f32[64,2048]{1,0:T(8,128)S(1)} fusion(s32[2048]{0:T(1024)} %bitcast.9), kind=kLoop, calls=%fused_computation.8 | loop fusion | flops 262144 | bytes 532480 | tf_op jit(solution)/shard_map/convert_element_type | solution.py:254
  0.8 1.6 %fusion = f32[2,64,128]{2,1,0:T(8,128)S(1)} fusion(s32[2048]{0:T(1024)} %param.8, f32[64,2048]{1,0:T(8,128)S(1)} %fusion.7, f32[2,2048]{1,0:T(2,128)} %param.6), kind=kOutput, calls=%fused_computation.1 | convolution fusion | flops 403177472 | bytes 614400 | tf_op jit(solution)/shard_map/dot_general | solution.py:261
  2.3 0.1 copy.13
  2.4 0.7 %pad_maximum_fusion.1 = f32[4,128]{1,0:T(4,128)S(1)} fusion(f32[1,128]{1,0:T(1,128)} %bitcast.10, f32[3,128]{1,0:T(4,128)} %param.9), kind=kLoop, calls=%fused_computation.12 | loop fusion | flops 512 | bytes 4096 | tf_op jit(solution)/shard_map/concatenate | solution.py:265
  3.1 0.1 pad_maximum_fusion
  3.2 29.8 %all_to_all.15.panel_ref = f32[64,6,128]{2,1,0:T(8,128)S(1)} all-to-all(f32[64,6,128]{2,1,0:T(8,128)S(1)} %pad_maximum_fusion), channel_id=1, replica_groups=mesh['panel'=64,'point'=8] {'panel'}, dimensions={0} | all-to-all | bytes 393216 | tf_op jit(solution)/shard_map/all_to_all | solution.py:268
  33.0 0.1 slice_reduce_fusion
  33.0 11.8 %all_to_all.16 = f32[8,2,128]{2,1,0:T(2,128)S(1)} all-to-all(f32[8,2,128]{2,1,0:T(2,128)S(1)} %broadcast_in_dim.10), channel_id=1, replica_groups=mesh['panel'=64,'point'=8] {'point'}, dimensions={0} | all-to-all | bytes 16384 | tf_op jit(solution)/shard_map/all_to_all | solution.py:274
  44.8 0.6 broadcast_in_dim.11
  45.5 4.6 %all-to-all-start.2 = ((f32[64,2,128]{2,1,0:T(2,128)}), f32[64,2,128]{2,1,0:T(2,128)S(1)}, u32[]{:S(2)}, u32[]{:S(2)}) async-start(f32[64,2,128]{2,1,0:T(2,128)} %broadcast_in_dim.11), calls=%async_computation.2 | async-start | bytes 131072 | tf_op jit(solution)/shard_map/all_to_all | solution.py:276
  50.1 0.0 copy-done.2
  50.1 3.4 %shard_map.64 = (f32[16,128,128]{2,1,0:T(8,128)}, f32[16,128,128]{2,1,0:T(8,128)}) custom-call(f32[64,6,128]{2,1,0:T(8,128)S(1)} %all_to_all.15.panel_ref, f32[3,128]{1,0:T(4,128)S(1)} %copy-done.2), custom_call_target="tpu_custom_call" | custom-call | flops 15728640 | bytes 2097152 | tf_op jit(solution)/shard_map/pallas_call | solution.py:208
  53.5 0.0 copy-start
  53.5 0.0 copy-start.1
  53.5 6.8 %shard_map.65 = (f32[40,128,128]{2,1,0:T(8,128)}, f32[40,128,128]{2,1,0:T(8,128)}) custom-call(f32[64,6,128]{2,1,0:T(8,128)S(1)} %all_to_all.15.panel_ref, f32[3,128]{1,0:T(4,128)S(1)} %copy-done.2), custom_call_target="tpu_custom_call" | custom-call | flops 39321600 | bytes 5242880 | tf_op jit(solution)/shard_map/pallas_call | solution.py:208
  60.3 0.9 %all-to-all-done.2.velocity_ref = f32[64,2,128]{2,1,0:T(2,128)S(1)} async-done(((f32[64,2,128]{2,1,0:T(2,128)}), f32[64,2,128]{2,1,0:T(2,128)S(1)}, u32[]{:S(2)}, u32[]{:S(2)}) %all-to-all-start.2) | async-done | bytes 65568 | tf_op jit(solution)/shard_map/all_to_all | solution.py:276
  61.2 0.0 copy-done
  61.2 0.0 copy-done.1
  61.2 3.6 %shard_map.66 = f32[2,128]{1,0:T(2,128)} custom-call(f32[64,2,128]{2,1,0:T(2,128)S(1)} %all-to-all-done.2.velocity_ref, f32[64,1,128]{2,1,0:T(1,128)S(1)} %slice.9.area_ref, f32[64,6,128]{2,1,0:T(8,128)S(1)} %all_to_all.15.panel_ref, f32[3,128]{1,0:T(4,128)S(1)} %copy-done.2, f32[16,128,128]{2,1,0:T(8,128)S(1)} %copy-done, f32[16,128,128]{2,1,0:T(8,128)S(1)} %copy-done.1, ...), custom_call_target="tpu_custom_call" | custom-call | flops 16515072 | bytes 5242880 | tf_op jit(solution)/shard_map/pallas_call | solution.py:230
  (4 shorter events, 0.1 us)
Async XLA Ops:
  0.0 50.1 %copy-start.2 = (f32[3,128]{1,0:T(4,128)S(1)}, f32[3,128]{1,0:T(4,128)}, u32[]{:S(2)}) copy-start(f32[3,128]{1,0:T(4,128)} %coordinate_ref.5) | copy-start | bytes 4612
  45.5 15.8 %all-to-all-start.2 = ((f32[64,2,128]{2,1,0:T(2,128)}), f32[64,2,128]{2,1,0:T(2,128)S(1)}, u32[]{:S(2)}, u32[]{:S(2)}) async-start(f32[64,2,128]{2,1,0:T(2,128)} %broadcast_in_dim.11), calls=%async_computation.2 | async-start | bytes 131072 | tf_op jit(solution)/shard_map/all_to_all | solution.py:276
  53.5 7.7 %copy-start = (f32[16,128,128]{2,1,0:T(8,128)S(1)}, f32[16,128,128]{2,1,0:T(8,128)}, u32[]{:S(2)}) copy-start(f32[16,128,128]{2,1,0:T(8,128)} %get-tuple-element.9.cosine_near) | copy-start | bytes 3145732
  53.5 7.7 %copy-start.1 = (f32[16,128,128]{2,1,0:T(8,128)S(1)}, f32[16,128,128]{2,1,0:T(8,128)}, u32[]{:S(2)}) copy-start(f32[16,128,128]{2,1,0:T(8,128)} %get-tuple-element.10.sine_near) | copy-start | bytes 3145732

commit v9 on v8

--- a/solution.py
+++ b/solution.py
@@ -262,9 +262,9 @@
         weighted, panel_hot, precision=lax.Precision.HIGHEST, preferred_element_type=jnp.float32
     )
     partial = partial.reshape(2, slab_count, slab_width).transpose(1, 0, 2)
-    extra = jnp.concatenate([panel_centroid, panel_area[None]], axis=0)
-    extra_copies = jnp.broadcast_to(extra[None], (slab_count,) + extra.shape)
-    outgoing = jnp.concatenate([partial, extra_copies], axis=1)
+    centroid_copies = jnp.broadcast_to(panel_centroid[None], (slab_count,) + panel_centroid.shape)
+    area_copies = jnp.broadcast_to(panel_area[None, None], (slab_count, 1, slab_width))
+    outgoing = jnp.concatenate([partial, centroid_copies, area_copies], axis=1)
     got = lax.all_to_all(outgoing, "panel", split_axis=0, concat_axis=0, tiled=True)
     near_parts = kernel_parts(got, field_points, 0, NEAR_CHUNKS)
     far_parts = kernel_parts(got, field_points, NEAR_CHUNKS, FAR_CHUNKS)

time: 65.3 us -> 66 us (1.011)
  local copies, waits for them, and re-layouts: 0.77 us -> 2.13 us
  other arithmetic: 1.61 us -> 0.93 us
    broadcast_in_dim x1 -> x2, local copies, waits for them, and re-layouts: 0.02 us -> 1.38 us  [the longest x1 0.7 us: shards(): jnp.broadcast_to(panel_centroid[None], (slab_count,) + panel_centroid.shape)]
    concatenate x2 -> x1, other arithmetic: 0.76 us -> 0.09 us  [shards(): outgoing = jnp.concatenate([partial, centroid_copies, area_copies], axis=1)]
where the time goes in v9:
time: 66 us; the launch traced here: 65.5 us
  blocking collectives  41.5 us (63%)
  Pallas kernels  13.8 us (21%)
  starting transfers between devices  4.6 us (7%)
  local copies, waits for them, and re-layouts  2.13 us (3%)
  matrix products  1.57 us (2%)
  other arithmetic  0.93 us (1%)
  waiting for transfers between devices  0.89 us (1%)
    all_to_all x1, blocking collectives, shards(): lax.all_to_all(outgoing, 'panel', split_axis=0, concat_axis=0, tiled=True)  29.8 us
    all_to_all x1, blocking collectives, shards(): lax.all_to_all(copies, 'point', split_axis=0, concat_axis=0, tiled=True)  11.8 us
    pallas_call x2, Pallas kernels, kernel_parts(): pl.pallas_call(functools.partial(parts_kernel, offset), out_shape=(part,...  10.2 us
    all_to_all x1, starting transfers between devices, shards(): lax.all_to_all(spread, 'panel', split_axis=0, concat_axis=0, tiled=True)  4.6 us
    pallas_call x1, Pallas kernels, finish(): pl.pallas_call(finish_kernel, out_shape=jax.ShapeDtypeStruct((2, points),...  3.59 us
    dot_general x1, matrix products, shards(): jnp.dot(weighted, panel_hot, precision=lax.Precision.HIGHEST, preferred_e...  1.57 us
  transfers between devices with their start and end apart: 1, of which 1 were waited for; matrix products, arithmetic and copies ran while one was open for 0% of the time, Pallas kernels for 16%

profile of v9, /device:TPU:1, one launch (start us, length us, event | category | flops | bytes accessed | tf_op | source)
XLA Modules:
  0.0 65.5 jit_solution(11790176118294028159)
XLA Ops:
  0.0 0.0 copy-start.2
  0.0 0.7 %fusion.7 = f32[64,2048]{1,0:T(8,128)S(1)} fusion(s32[2048]{0:T(1024)} %bitcast.8), kind=kLoop, calls=%fused_computation.8 | loop fusion | flops 262144 | bytes 532480 | tf_op jit(solution)/shard_map/convert_element_type | solution.py:254
  0.8 1.6 %fusion = f32[2,64,128]{2,1,0:T(8,128)S(1)} fusion(s32[2048]{0:T(1024)} %param.8, f32[64,2048]{1,0:T(8,128)S(1)} %fusion.7, f32[2,2048]{1,0:T(2,128)} %param.6), kind=kOutput, calls=%fused_computation.1 | convolution fusion | flops 403177472 | bytes 614400 | tf_op jit(solution)/shard_map/dot_general | solution.py:261
  2.3 0.1 copy.13
  2.4 0.7 %broadcast_in_dim.9 = f32[64,1,128]{2,1,0:T(1,128)S(1)} broadcast(f32[128]{0:T(128)} %param.10), dimensions={2} | broadcast | bytes 33280 | tf_op jit(solution)/shard_map/broadcast_in_dim | solution.py:266
  3.1 0.7 %broadcast_in_dim.8 = f32[64,3,128]{2,1,0:T(4,128)S(1)} broadcast(f32[3,128]{1,0:T(4,128)} %param.9), dimensions={1,2} | broadcast | bytes 99840 | tf_op jit(solution)/shard_map/broadcast_in_dim | solution.py:265
  3.8 0.1 pad_maximum_fusion
  3.9 29.8 %all_to_all.15.panel_ref = f32[64,6,128]{2,1,0:T(8,128)S(1)} all-to-all(f32[64,6,128]{2,1,0:T(8,128)S(1)} %pad_maximum_fusion), channel_id=1, replica_groups=mesh['panel'=64,'point'=8] {'panel'}, dimensions={0} | all-to-all | bytes 393216 | tf_op jit(solution)/shard_map/all_to_all | solution.py:268
  33.6 0.1 slice_reduce_fusion
  33.7 11.8 %all_to_all.16 = f32[8,2,128]{2,1,0:T(2,128)S(1)} all-to-all(f32[8,2,128]{2,1,0:T(2,128)S(1)} %broadcast_in_dim.10), channel_id=1, replica_groups=mesh['panel'=64,'point'=8] {'point'}, dimensions={0} | all-to-all | bytes 16384 | tf_op jit(solution)/shard_map/all_to_all | solution.py:274
  45.5 0.6 broadcast_in_dim.11
  46.1 4.6 %all-to-all-start.2 = ((f32[64,2,128]{2,1,0:T(2,128)}), f32[64,2,128]{2,1,0:T(2,128)S(1)}, u32[]{:S(2)}, u32[]{:S(2)}) async-start(f32[64,2,128]{2,1,0:T(2,128)} %broadcast_in_dim.11), calls=%async_computation.2 | async-start | bytes 131072 | tf_op jit(solution)/shard_map/all_to_all | solution.py:276
  50.8 0.0 copy-done.2
  50.8 3.4 %shard_map.64 = (f32[16,128,128]{2,1,0:T(8,128)}, f32[16,128,128]{2,1,0:T(8,128)}) custom-call(f32[64,6,128]{2,1,0:T(8,128)S(1)} %all_to_all.15.panel_ref, f32[3,128]{1,0:T(4,128)S(1)} %copy-done.2), custom_call_target="tpu_custom_call" | custom-call | flops 15728640 | bytes 2097152 | tf_op jit(solution)/shard_map/pallas_call | solution.py:208
  54.2 0.0 copy-start
  54.2 0.0 copy-start.1
  54.2 6.8 %shard_map.65 = (f32[40,128,128]{2,1,0:T(8,128)}, f32[40,128,128]{2,1,0:T(8,128)}) custom-call(f32[64,6,128]{2,1,0:T(8,128)S(1)} %all_to_all.15.panel_ref, f32[3,128]{1,0:T(4,128)S(1)} %copy-done.2), custom_call_target="tpu_custom_call" | custom-call | flops 39321600 | bytes 5242880 | tf_op jit(solution)/shard_map/pallas_call | solution.py:208
  61.0 0.9 %all-to-all-done.2.velocity_ref = f32[64,2,128]{2,1,0:T(2,128)S(1)} async-done(((f32[64,2,128]{2,1,0:T(2,128)}), f32[64,2,128]{2,1,0:T(2,128)S(1)}, u32[]{:S(2)}, u32[]{:S(2)}) %all-to-all-start.2) | async-done | bytes 65568 | tf_op jit(solution)/shard_map/all_to_all | solution.py:276
  61.9 0.0 copy-done
  61.9 0.0 copy-done.1
  61.9 3.6 %shard_map.66 = f32[2,128]{1,0:T(2,128)} custom-call(f32[64,2,128]{2,1,0:T(2,128)S(1)} %all-to-all-done.2.velocity_ref, f32[64,1,128]{2,1,0:T(1,128)S(1)} %slice.9.area_ref, f32[64,6,128]{2,1,0:T(8,128)S(1)} %all_to_all.15.panel_ref, f32[3,128]{1,0:T(4,128)S(1)} %copy-done.2, f32[16,128,128]{2,1,0:T(8,128)S(1)} %copy-done, f32[16,128,128]{2,1,0:T(8,128)S(1)} %copy-done.1, ...), custom_call_target="tpu_custom_call" | custom-call | flops 16515072 | bytes 5242880 | tf_op jit(solution)/shard_map/pallas_call | solution.py:230
  (3 shorter events, 0.1 us)
Async XLA Ops:
  0.0 50.8 %copy-start.2 = (f32[3,128]{1,0:T(4,128)S(1)}, f32[3,128]{1,0:T(4,128)}, u32[]{:S(2)}) copy-start(f32[3,128]{1,0:T(4,128)} %coordinate_ref.5) | copy-start | bytes 4612
  46.1 15.8 %all-to-all-start.2 = ((f32[64,2,128]{2,1,0:T(2,128)}), f32[64,2,128]{2,1,0:T(2,128)S(1)}, u32[]{:S(2)}, u32[]{:S(2)}) async-start(f32[64,2,128]{2,1,0:T(2,128)} %broadcast_in_dim.11), calls=%async_computation.2 | async-start | bytes 131072 | tf_op jit(solution)/shard_map/all_to_all | solution.py:276
  54.2 7.7 %copy-start = (f32[16,128,128]{2,1,0:T(8,128)S(1)}, f32[16,128,128]{2,1,0:T(8,128)}, u32[]{:S(2)}) copy-start(f32[16,128,128]{2,1,0:T(8,128)} %get-tuple-element.9.cosine_near) | copy-start | bytes 3145732
  54.2 7.7 %copy-start.1 = (f32[16,128,128]{2,1,0:T(8,128)S(1)}, f32[16,128,128]{2,1,0:T(8,128)}, u32[]{:S(2)}) copy-start(f32[16,128,128]{2,1,0:T(8,128)} %get-tuple-element.10.sine_near) | copy-start | bytes 3145732

commit v10 on v8

--- a/solution.py
+++ b/solution.py
@@ -20,6 +20,7 @@
 PARTS_STEP = 8
 NEAR_CHUNKS = 16
 FAR_CHUNKS = 40
+FAR_COPY = 40
 
 
 def sine_cosine(angle):
@@ -133,10 +134,10 @@
     far = cosine_hbm.shape[0]
     chunks = panel_ref.shape[0]
     points = point_ref.shape[1]
-    groups = far // PARTS_STEP
+    groups = far // FAR_COPY
 
     def copies(group):
-        window = pl.ds(group * PARTS_STEP, PARTS_STEP)
+        window = pl.ds(group * FAR_COPY, FAR_COPY)
         return (
             pltpu.make_async_copy(cosine_hbm.at[window], cosine_buf.at[window], sems.at[0, group]),
             pltpu.make_async_copy(sine_hbm.at[window], sine_buf.at[window], sems.at[1, group]),
@@ -194,8 +195,8 @@
     for group in range(groups):
         for copy in copies(group):
             copy.wait()
-        start = near + group * PARTS_STEP
-        lax.fori_loop(start, start + PARTS_STEP, saved(cosine_buf, sine_buf, near), 0)
+        start = near + group * FAR_COPY
+        lax.fori_loop(start, start + FAR_COPY, saved(cosine_buf, sine_buf, near), 0)
     out_ref[0:1, :] = jnp.sum(real_ref[...].T, axis=0, keepdims=True)
     out_ref[1:2, :] = jnp.sum(imag_ref[...].T, axis=0, keepdims=True)
 
@@ -235,7 +236,7 @@
         scratch_shapes=[pltpu.VMEM((far, points, lanes), jnp.float32)] * 2
         + [pltpu.VMEM((3, points, lanes), jnp.float32)]
         + [pltpu.VMEM((points, lanes), jnp.float32)] * 2
-        + [pltpu.SemaphoreType.DMA((2, far // PARTS_STEP))],
+        + [pltpu.SemaphoreType.DMA((2, far // FAR_COPY))],
         cost_estimate=pl.CostEstimate(
             flops=70 * pairs + 8 * stored * points * lanes,
             transcendentals=2 * pairs,

time: 65.3 us -> 65.9 us (level)
  no operation moved by 1% of the time
where the time goes in v10:
time: 65.9 us; the launch traced here: 65.4 us
  blocking collectives  41.5 us (63%)
  Pallas kernels  14.4 us (22%)
  starting transfers between devices  4.6 us (7%)
  other arithmetic  1.61 us (2%)
  matrix products  1.57 us (2%)
  waiting for transfers between devices  0.89 us (1%)
  local copies, waits for them, and re-layouts  0.77 us (1%)
    all_to_all x1, blocking collectives, shards(): lax.all_to_all(outgoing, 'panel', split_axis=0, concat_axis=0, tiled=True)  29.8 us
    all_to_all x1, blocking collectives, shards(): lax.all_to_all(copies, 'point', split_axis=0, concat_axis=0, tiled=True)  11.8 us
    pallas_call x2, Pallas kernels, kernel_parts(): pl.pallas_call(functools.partial(parts_kernel, offset), out_shape=(part,...  10.2 us
    all_to_all x1, starting transfers between devices, shards(): lax.all_to_all(spread, 'panel', split_axis=0, concat_axis=0, tiled=True)  4.6 us
    pallas_call x1, Pallas kernels, finish(): pl.pallas_call(finish_kernel, out_shape=jax.ShapeDtypeStruct((2, points),...  4.23 us
    dot_general x1, matrix products, shards(): jnp.dot(weighted, panel_hot, precision=lax.Precision.HIGHEST, preferred_e...  1.57 us
  transfers between devices with their start and end apart: 1, of which 1 were waited for; matrix products, arithmetic and copies ran while one was open for 0% of the time, Pallas kernels for 16%

profile of v10, /device:TPU:1, one launch (start us, length us, event | category | flops | bytes accessed | tf_op | source)
XLA Modules:
  0.0 65.4 jit_solution(11839731292683332193)
XLA Ops:
  0.0 0.0 copy-start.2
  0.0 0.7 %fusion.7 = f32[64,2048]{1,0:T(8,128)S(1)} fusion(s32[2048]{0:T(1024)} %bitcast.9), kind=kLoop, calls=%fused_computation.8 | loop fusion | flops 262144 | bytes 532480 | tf_op jit(solution)/shard_map/convert_element_type | solution.py:255
  0.8 1.6 %fusion = f32[2,64,128]{2,1,0:T(8,128)S(1)} fusion(s32[2048]{0:T(1024)} %param.8, f32[64,2048]{1,0:T(8,128)S(1)} %fusion.7, f32[2,2048]{1,0:T(2,128)} %param.6), kind=kOutput, calls=%fused_computation.1 | convolution fusion | flops 403177472 | bytes 614400 | tf_op jit(solution)/shard_map/dot_general | solution.py:262
  2.3 0.1 copy.13
  2.4 0.7 %pad_maximum_fusion.1 = f32[4,128]{1,0:T(4,128)S(1)} fusion(f32[1,128]{1,0:T(1,128)} %bitcast.10, f32[3,128]{1,0:T(4,128)} %param.9), kind=kLoop, calls=%fused_computation.12 | loop fusion | flops 512 | bytes 4096 | tf_op jit(solution)/shard_map/concatenate | solution.py:266
  3.1 0.1 pad_maximum_fusion
  3.2 29.8 %all_to_all.15.panel_ref = f32[64,6,128]{2,1,0:T(8,128)S(1)} all-to-all(f32[64,6,128]{2,1,0:T(8,128)S(1)} %pad_maximum_fusion), channel_id=1, replica_groups=mesh['panel'=64,'point'=8] {'panel'}, dimensions={0} | all-to-all | bytes 393216 | tf_op jit(solution)/shard_map/all_to_all | solution.py:269
  33.0 0.1 slice_reduce_fusion
  33.0 11.8 %all_to_all.16 = f32[8,2,128]{2,1,0:T(2,128)S(1)} all-to-all(f32[8,2,128]{2,1,0:T(2,128)S(1)} %broadcast_in_dim.10), channel_id=1, replica_groups=mesh['panel'=64,'point'=8] {'point'}, dimensions={0} | all-to-all | bytes 16384 | tf_op jit(solution)/shard_map/all_to_all | solution.py:275
  44.8 0.6 broadcast_in_dim.11
  45.5 4.6 %all-to-all-start.2 = ((f32[64,2,128]{2,1,0:T(2,128)}), f32[64,2,128]{2,1,0:T(2,128)S(1)}, u32[]{:S(2)}, u32[]{:S(2)}) async-start(f32[64,2,128]{2,1,0:T(2,128)} %broadcast_in_dim.11), calls=%async_computation.2 | async-start | bytes 131072 | tf_op jit(solution)/shard_map/all_to_all | solution.py:277
  50.1 0.0 copy-done.2
  50.1 3.4 %shard_map.64 = (f32[16,128,128]{2,1,0:T(8,128)}, f32[16,128,128]{2,1,0:T(8,128)}) custom-call(f32[64,6,128]{2,1,0:T(8,128)S(1)} %all_to_all.15.panel_ref, f32[3,128]{1,0:T(4,128)S(1)} %copy-done.2), custom_call_target="tpu_custom_call" | custom-call | flops 15728640 | bytes 2097152 | tf_op jit(solution)/shard_map/pallas_call | solution.py:209
  53.5 0.0 copy-start
  53.5 0.0 copy-start.1
  53.5 6.8 %shard_map.65 = (f32[40,128,128]{2,1,0:T(8,128)}, f32[40,128,128]{2,1,0:T(8,128)}) custom-call(f32[64,6,128]{2,1,0:T(8,128)S(1)} %all_to_all.15.panel_ref, f32[3,128]{1,0:T(4,128)S(1)} %copy-done.2), custom_call_target="tpu_custom_call" | custom-call | flops 39321600 | bytes 5242880 | tf_op jit(solution)/shard_map/pallas_call | solution.py:209
  60.3 0.9 %all-to-all-done.2.velocity_ref = f32[64,2,128]{2,1,0:T(2,128)S(1)} async-done(((f32[64,2,128]{2,1,0:T(2,128)}), f32[64,2,128]{2,1,0:T(2,128)S(1)}, u32[]{:S(2)}, u32[]{:S(2)}) %all-to-all-start.2) | async-done | bytes 65568 | tf_op jit(solution)/shard_map/all_to_all | solution.py:277
  61.2 0.0 copy-done
  61.2 0.0 copy-done.1
  61.2 4.2 %shard_map.66 = f32[2,128]{1,0:T(2,128)} custom-call(f32[64,2,128]{2,1,0:T(2,128)S(1)} %all-to-all-done.2.velocity_ref, f32[64,1,128]{2,1,0:T(1,128)S(1)} %slice.9.area_ref, f32[64,6,128]{2,1,0:T(8,128)S(1)} %all_to_all.15.panel_ref, f32[3,128]{1,0:T(4,128)S(1)} %copy-done.2, f32[16,128,128]{2,1,0:T(8,128)S(1)} %copy-done, f32[16,128,128]{2,1,0:T(8,128)S(1)} %copy-done.1, ...), custom_call_target="tpu_custom_call" | custom-call | flops 16515072 | bytes 5242880 | tf_op jit(solution)/shard_map/pallas_call | solution.py:231
  (4 shorter events, 0.1 us)
Async XLA Ops:
  0.0 50.1 %copy-start.2 = (f32[3,128]{1,0:T(4,128)S(1)}, f32[3,128]{1,0:T(4,128)}, u32[]{:S(2)}) copy-start(f32[3,128]{1,0:T(4,128)} %coordinate_ref.5) | copy-start | bytes 4612
  45.5 15.8 %all-to-all-start.2 = ((f32[64,2,128]{2,1,0:T(2,128)}), f32[64,2,128]{2,1,0:T(2,128)S(1)}, u32[]{:S(2)}, u32[]{:S(2)}) async-start(f32[64,2,128]{2,1,0:T(2,128)} %broadcast_in_dim.11), calls=%async_computation.2 | async-start | bytes 131072 | tf_op jit(solution)/shard_map/all_to_all | solution.py:277
  53.5 7.7 %copy-start = (f32[16,128,128]{2,1,0:T(8,128)S(1)}, f32[16,128,128]{2,1,0:T(8,128)}, u32[]{:S(2)}) copy-start(f32[16,128,128]{2,1,0:T(8,128)} %get-tuple-element.9.cosine_near) | copy-start | bytes 3145732
  53.5 7.7 %copy-start.1 = (f32[16,128,128]{2,1,0:T(8,128)S(1)}, f32[16,128,128]{2,1,0:T(8,128)}, u32[]{:S(2)}) copy-start(f32[16,128,128]{2,1,0:T(8,128)} %get-tuple-element.10.sine_near) | copy-start | bytes 3145732

commit v11 on v8

--- a/solution.py
+++ b/solution.py
@@ -259,7 +259,7 @@
         jnp.float32
     )
     partial = jnp.dot(
-        weighted, panel_hot, precision=lax.Precision.HIGHEST, preferred_element_type=jnp.float32
+        weighted, panel_hot, precision=lax.Precision.HIGH, preferred_element_type=jnp.float32
     )
     partial = partial.reshape(2, slab_count, slab_width).transpose(1, 0, 2)
     extra = jnp.concatenate([panel_centroid, panel_area[None]], axis=0)

time: 65.3 us -> 65.1 us (level)
  no operation moved by 1% of the time
where the time goes in v11:
time: 65.1 us; the launch traced here: 64.6 us
  blocking collectives  41.5 us (64%)
  Pallas kernels  13.8 us (21%)
  starting transfers between devices  4.6 us (7%)
  other arithmetic  1.61 us (2%)
  matrix products  1.39 us (2%)
  waiting for transfers between devices  0.89 us (1%)
  local copies, waits for them, and re-layouts  0.77 us (1%)
    all_to_all x1, blocking collectives, shards(): lax.all_to_all(outgoing, 'panel', split_axis=0, concat_axis=0, tiled=True)  29.8 us
    all_to_all x1, blocking collectives, shards(): lax.all_to_all(copies, 'point', split_axis=0, concat_axis=0, tiled=True)  11.7 us
    pallas_call x2, Pallas kernels, kernel_parts(): pl.pallas_call(functools.partial(parts_kernel, offset), out_shape=(part,...  10.2 us
    all_to_all x1, starting transfers between devices, shards(): lax.all_to_all(spread, 'panel', split_axis=0, concat_axis=0, tiled=True)  4.6 us
    pallas_call x1, Pallas kernels, finish(): pl.pallas_call(finish_kernel, out_shape=jax.ShapeDtypeStruct((2, points),...  3.59 us
    dot_general x1, matrix products, shards(): jnp.dot(weighted, panel_hot, precision=lax.Precision.HIGH, preferred_elem...  1.39 us
  transfers between devices with their start and end apart: 1, of which 1 were waited for; matrix products, arithmetic and copies ran while one was open for 0% of the time, Pallas kernels for 16%

profile of v11, /device:TPU:1, one launch (start us, length us, event | category | flops | bytes accessed | tf_op | source)
XLA Modules:
  0.0 64.6 jit_solution(13465331060851863934)
XLA Ops:
  0.0 0.0 copy-start.2
  0.0 0.7 %fusion.7 = f32[64,2048]{1,0:T(8,128)S(1)} fusion(s32[2048]{0:T(1024)} %bitcast.9), kind=kLoop, calls=%fused_computation.8 | loop fusion | flops 262144 | bytes 532480 | tf_op jit(solution)/shard_map/convert_element_type | solution.py:254
  0.8 1.4 %fusion = f32[2,64,128]{2,1,0:T(8,128)S(1)} fusion(s32[2048]{0:T(1024)} %param.8, f32[64,2048]{1,0:T(8,128)S(1)} %fusion.7, f32[2,2048]{1,0:T(2,128)} %param.6), kind=kOutput, calls=%fused_computation.1 | convolution fusion | flops 201850880 | bytes 614400 | tf_op jit(solution)/shard_map/dot_general | solution.py:261
  2.2 0.1 copy.13
  2.2 0.7 %pad_maximum_fusion.1 = f32[4,128]{1,0:T(4,128)S(1)} fusion(f32[1,128]{1,0:T(1,128)} %bitcast.10, f32[3,128]{1,0:T(4,128)} %param.9), kind=kLoop, calls=%fused_computation.12 | loop fusion | flops 512 | bytes 4096 | tf_op jit(solution)/shard_map/concatenate | solution.py:265
  2.9 0.1 pad_maximum_fusion
  3.0 29.8 %all_to_all.15.panel_ref = f32[64,6,128]{2,1,0:T(8,128)S(1)} all-to-all(f32[64,6,128]{2,1,0:T(8,128)S(1)} %pad_maximum_fusion), channel_id=1, replica_groups=mesh['panel'=64,'point'=8] {'panel'}, dimensions={0} | all-to-all | bytes 393216 | tf_op jit(solution)/shard_map/all_to_all | solution.py:268
  32.8 0.1 slice_reduce_fusion
  32.9 11.7 %all_to_all.16 = f32[8,2,128]{2,1,0:T(2,128)S(1)} all-to-all(f32[8,2,128]{2,1,0:T(2,128)S(1)} %broadcast_in_dim.10), channel_id=1, replica_groups=mesh['panel'=64,'point'=8] {'point'}, dimensions={0} | all-to-all | bytes 16384 | tf_op jit(solution)/shard_map/all_to_all | solution.py:274
  44.6 0.6 broadcast_in_dim.11
  45.3 4.6 %all-to-all-start.2 = ((f32[64,2,128]{2,1,0:T(2,128)}), f32[64,2,128]{2,1,0:T(2,128)S(1)}, u32[]{:S(2)}, u32[]{:S(2)}) async-start(f32[64,2,128]{2,1,0:T(2,128)} %broadcast_in_dim.11), calls=%async_computation.2 | async-start | bytes 131072 | tf_op jit(solution)/shard_map/all_to_all | solution.py:276
  49.9 0.0 copy-done.2
  49.9 3.4 %shard_map.64 = (f32[16,128,128]{2,1,0:T(8,128)}, f32[16,128,128]{2,1,0:T(8,128)}) custom-call(f32[64,6,128]{2,1,0:T(8,128)S(1)} %all_to_all.15.panel_ref, f32[3,128]{1,0:T(4,128)S(1)} %copy-done.2), custom_call_target="tpu_custom_call" | custom-call | flops 15728640 | bytes 2097152 | tf_op jit(solution)/shard_map/pallas_call | solution.py:208
  53.3 0.0 copy-start
  53.3 0.0 copy-start.1
  53.3 6.8 %shard_map.65 = (f32[40,128,128]{2,1,0:T(8,128)}, f32[40,128,128]{2,1,0:T(8,128)}) custom-call(f32[64,6,128]{2,1,0:T(8,128)S(1)} %all_to_all.15.panel_ref, f32[3,128]{1,0:T(4,128)S(1)} %copy-done.2), custom_call_target="tpu_custom_call" | custom-call | flops 39321600 | bytes 5242880 | tf_op jit(solution)/shard_map/pallas_call | solution.py:208
  60.1 0.9 %all-to-all-done.2.velocity_ref = f32[64,2,128]{2,1,0:T(2,128)S(1)} async-done(((f32[64,2,128]{2,1,0:T(2,128)}), f32[64,2,128]{2,1,0:T(2,128)S(1)}, u32[]{:S(2)}, u32[]{:S(2)}) %all-to-all-start.2) | async-done | bytes 65568 | tf_op jit(solution)/shard_map/all_to_all | solution.py:276
  61.0 0.0 copy-done
  61.0 0.0 copy-done.1
  61.0 3.6 %shard_map.66 = f32[2,128]{1,0:T(2,128)} custom-call(f32[64,2,128]{2,1,0:T(2,128)S(1)} %all-to-all-done.2.velocity_ref, f32[64,1,128]{2,1,0:T(1,128)S(1)} %slice.9.area_ref, f32[64,6,128]{2,1,0:T(8,128)S(1)} %all_to_all.15.panel_ref, f32[3,128]{1,0:T(4,128)S(1)} %copy-done.2, f32[16,128,128]{2,1,0:T(8,128)S(1)} %copy-done, f32[16,128,128]{2,1,0:T(8,128)S(1)} %copy-done.1, ...), custom_call_target="tpu_custom_call" | custom-call | flops 16515072 | bytes 5242880 | tf_op jit(solution)/shard_map/pallas_call | solution.py:230
  (4 shorter events, 0.1 us)
Async XLA Ops:
  0.0 49.9 %copy-start.2 = (f32[3,128]{1,0:T(4,128)S(1)}, f32[3,128]{1,0:T(4,128)}, u32[]{:S(2)}) copy-start(f32[3,128]{1,0:T(4,128)} %coordinate_ref.5) | copy-start | bytes 4612
  45.3 15.8 %all-to-all-start.2 = ((f32[64,2,128]{2,1,0:T(2,128)}), f32[64,2,128]{2,1,0:T(2,128)S(1)}, u32[]{:S(2)}, u32[]{:S(2)}) async-start(f32[64,2,128]{2,1,0:T(2,128)} %broadcast_in_dim.11), calls=%async_computation.2 | async-start | bytes 131072 | tf_op jit(solution)/shard_map/all_to_all | solution.py:276
  53.3 7.7 %copy-start = (f32[16,128,128]{2,1,0:T(8,128)S(1)}, f32[16,128,128]{2,1,0:T(8,128)}, u32[]{:S(2)}) copy-start(f32[16,128,128]{2,1,0:T(8,128)} %get-tuple-element.9.cosine_near) | copy-start | bytes 3145732
  53.3 7.7 %copy-start.1 = (f32[16,128,128]{2,1,0:T(8,128)S(1)}, f32[16,128,128]{2,1,0:T(8,128)}, u32[]{:S(2)}) copy-start(f32[16,128,128]{2,1,0:T(8,128)} %get-tuple-element.10.sine_near) | copy-start | bytes 3145732

commit v12 on v8

--- a/solution.py
+++ b/solution.py
@@ -190,12 +190,12 @@
 
         return body
 
-    lax.fori_loop(0, near, saved(cosine_near, sine_near, 0), 0)
+    lax.fori_loop(0, near, saved(cosine_near, sine_near, 0), 0, unroll=2)
     for group in range(groups):
         for copy in copies(group):
             copy.wait()
         start = near + group * PARTS_STEP
-        lax.fori_loop(start, start + PARTS_STEP, saved(cosine_buf, sine_buf, near), 0)
+        lax.fori_loop(start, start + PARTS_STEP, saved(cosine_buf, sine_buf, near), 0, unroll=2)
     out_ref[0:1, :] = jnp.sum(real_ref[...].T, axis=0, keepdims=True)
     out_ref[1:2, :] = jnp.sum(imag_ref[...].T, axis=0, keepdims=True)
 

time: 65.3 us -> 65.2 us (level)
  no operation moved by 1% of the time
where the time goes in v12:
time: 65.2 us; the launch traced here: 64.7 us
  blocking collectives  41.5 us (64%)
  Pallas kernels  13.7 us (21%)
  starting transfers between devices  4.6 us (7%)
  other arithmetic  1.61 us (2%)
  matrix products  1.57 us (2%)
  waiting for transfers between devices  0.89 us (1%)
  local copies, waits for them, and re-layouts  0.77 us (1%)
    all_to_all x1, blocking collectives, shards(): lax.all_to_all(outgoing, 'panel', split_axis=0, concat_axis=0, tiled=True)  29.8 us
    all_to_all x1, blocking collectives, shards(): lax.all_to_all(copies, 'point', split_axis=0, concat_axis=0, tiled=True)  11.8 us
    pallas_call x2, Pallas kernels, kernel_parts(): pl.pallas_call(functools.partial(parts_kernel, offset), out_shape=(part,...  10.2 us
    all_to_all x1, starting transfers between devices, shards(): lax.all_to_all(spread, 'panel', split_axis=0, concat_axis=0, tiled=True)  4.6 us
    pallas_call x1, Pallas kernels, finish(): pl.pallas_call(finish_kernel, out_shape=jax.ShapeDtypeStruct((2, points),...  3.49 us
    dot_general x1, matrix products, shards(): jnp.dot(weighted, panel_hot, precision=lax.Precision.HIGHEST, preferred_e...  1.57 us
  transfers between devices with their start and end apart: 1, of which 1 were waited for; matrix products, arithmetic and copies ran while one was open for 0% of the time, Pallas kernels for 16%

profile of v12, /device:TPU:1, one launch (start us, length us, event | category | flops | bytes accessed | tf_op | source)
XLA Modules:
  0.0 64.7 jit_solution(14249285052645549794)
XLA Ops:
  0.0 0.0 copy-start.2
  0.0 0.7 %fusion.7 = f32[64,2048]{1,0:T(8,128)S(1)} fusion(s32[2048]{0:T(1024)} %bitcast.9), kind=kLoop, calls=%fused_computation.8 | loop fusion | flops 262144 | bytes 532480 | tf_op jit(solution)/shard_map/convert_element_type | solution.py:254
  0.8 1.6 %fusion = f32[2,64,128]{2,1,0:T(8,128)S(1)} fusion(s32[2048]{0:T(1024)} %param.8, f32[64,2048]{1,0:T(8,128)S(1)} %fusion.7, f32[2,2048]{1,0:T(2,128)} %param.6), kind=kOutput, calls=%fused_computation.1 | convolution fusion | flops 403177472 | bytes 614400 | tf_op jit(solution)/shard_map/dot_general | solution.py:261
  2.3 0.1 copy.13
  2.4 0.7 %pad_maximum_fusion.1 = f32[4,128]{1,0:T(4,128)S(1)} fusion(f32[1,128]{1,0:T(1,128)} %bitcast.10, f32[3,128]{1,0:T(4,128)} %param.9), kind=kLoop, calls=%fused_computation.12 | loop fusion | flops 512 | bytes 4096 | tf_op jit(solution)/shard_map/concatenate | solution.py:265
  3.1 0.1 pad_maximum_fusion
  3.2 29.8 %all_to_all.15.panel_ref = f32[64,6,128]{2,1,0:T(8,128)S(1)} all-to-all(f32[64,6,128]{2,1,0:T(8,128)S(1)} %pad_maximum_fusion), channel_id=1, replica_groups=mesh['panel'=64,'point'=8] {'panel'}, dimensions={0} | all-to-all | bytes 393216 | tf_op jit(solution)/shard_map/all_to_all | solution.py:268
  33.0 0.1 slice_reduce_fusion
  33.0 11.8 %all_to_all.16 = f32[8,2,128]{2,1,0:T(2,128)S(1)} all-to-all(f32[8,2,128]{2,1,0:T(2,128)S(1)} %broadcast_in_dim.10), channel_id=1, replica_groups=mesh['panel'=64,'point'=8] {'point'}, dimensions={0} | all-to-all | bytes 16384 | tf_op jit(solution)/shard_map/all_to_all | solution.py:274
  44.8 0.6 broadcast_in_dim.11
  45.5 4.6 %all-to-all-start.2 = ((f32[64,2,128]{2,1,0:T(2,128)}), f32[64,2,128]{2,1,0:T(2,128)S(1)}, u32[]{:S(2)}, u32[]{:S(2)}) async-start(f32[64,2,128]{2,1,0:T(2,128)} %broadcast_in_dim.11), calls=%async_computation.2 | async-start | bytes 131072 | tf_op jit(solution)/shard_map/all_to_all | solution.py:276
  50.1 0.0 copy-done.2
  50.1 3.4 %shard_map.64 = (f32[16,128,128]{2,1,0:T(8,128)}, f32[16,128,128]{2,1,0:T(8,128)}) custom-call(f32[64,6,128]{2,1,0:T(8,128)S(1)} %all_to_all.15.panel_ref, f32[3,128]{1,0:T(4,128)S(1)} %copy-done.2), custom_call_target="tpu_custom_call" | custom-call | flops 15728640 | bytes 2097152 | tf_op jit(solution)/shard_map/pallas_call | solution.py:208
  53.5 0.0 copy-start
  53.5 0.0 copy-start.1
  53.5 6.8 %shard_map.65 = (f32[40,128,128]{2,1,0:T(8,128)}, f32[40,128,128]{2,1,0:T(8,128)}) custom-call(f32[64,6,128]{2,1,0:T(8,128)S(1)} %all_to_all.15.panel_ref, f32[3,128]{1,0:T(4,128)S(1)} %copy-done.2), custom_call_target="tpu_custom_call" | custom-call | flops 39321600 | bytes 5242880 | tf_op jit(solution)/shard_map/pallas_call | solution.py:208
  60.3 0.9 %all-to-all-done.2.velocity_ref = f32[64,2,128]{2,1,0:T(2,128)S(1)} async-done(((f32[64,2,128]{2,1,0:T(2,128)}), f32[64,2,128]{2,1,0:T(2,128)S(1)}, u32[]{:S(2)}, u32[]{:S(2)}) %all-to-all-start.2) | async-done | bytes 65568 | tf_op jit(solution)/shard_map/all_to_all | solution.py:276
  61.2 0.0 copy-done
  61.2 0.0 copy-done.1
  61.2 3.5 %shard_map.66 = f32[2,128]{1,0:T(2,128)} custom-call(f32[64,2,128]{2,1,0:T(2,128)S(1)} %all-to-all-done.2.velocity_ref, f32[64,1,128]{2,1,0:T(1,128)S(1)} %slice.9.area_ref, f32[64,6,128]{2,1,0:T(8,128)S(1)} %all_to_all.15.panel_ref, f32[3,128]{1,0:T(4,128)S(1)} %copy-done.2, f32[16,128,128]{2,1,0:T(8,128)S(1)} %copy-done, f32[16,128,128]{2,1,0:T(8,128)S(1)} %copy-done.1, ...), custom_call_target="tpu_custom_call" | custom-call | flops 16515072 | bytes 5242880 | tf_op jit(solution)/shard_map/pallas_call | solution.py:230
  (4 shorter events, 0.1 us)
Async XLA Ops:
  0.0 50.1 %copy-start.2 = (f32[3,128]{1,0:T(4,128)S(1)}, f32[3,128]{1,0:T(4,128)}, u32[]{:S(2)}) copy-start(f32[3,128]{1,0:T(4,128)} %coordinate_ref.5) | copy-start | bytes 4612
  45.5 15.8 %all-to-all-start.2 = ((f32[64,2,128]{2,1,0:T(2,128)}), f32[64,2,128]{2,1,0:T(2,128)S(1)}, u32[]{:S(2)}, u32[]{:S(2)}) async-start(f32[64,2,128]{2,1,0:T(2,128)} %broadcast_in_dim.11), calls=%async_computation.2 | async-start | bytes 131072 | tf_op jit(solution)/shard_map/all_to_all | solution.py:276
  53.5 7.7 %copy-start = (f32[16,128,128]{2,1,0:T(8,128)S(1)}, f32[16,128,128]{2,1,0:T(8,128)}, u32[]{:S(2)}) copy-start(f32[16,128,128]{2,1,0:T(8,128)} %get-tuple-element.9.cosine_near) | copy-start | bytes 3145732
  53.5 7.7 %copy-start.1 = (f32[16,128,128]{2,1,0:T(8,128)S(1)}, f32[16,128,128]{2,1,0:T(8,128)}, u32[]{:S(2)}) copy-start(f32[16,128,128]{2,1,0:T(8,128)} %get-tuple-element.10.sine_near) | copy-start | bytes 3145732
